TPU v7x, 256 devices: a whole 4x4x8 slice. The times are simulated.
256 devices in a mesh: section: 4 (over x_hi, core), expert: 4 (over y), dp: 16 (over z, x_lo).
Axes of the slice: x: 4 (x_hi: 2, x_lo: 2; x = x_hi * 2 + x_lo), y: 4, z: 8, core: 2. Of those that a mesh axis runs over, the one named last changes fastest.
Arguments:
- tokens: bfloat16 [2, 4096, 3072], P(None, ('expert', 'dp')), may hold values from -6 to 6
- routes: int32 [2, 4096, 2], P(None, ('expert', 'dp')), may hold values from 0 to 3, all different within a row; in each aligned block of 64 rows (0 to 63, 64 to 127, ..., all dimensions but the last counted through in order) at most 36 rows name the same one
- router: bfloat16 [3072, 4], replicated, may hold values from -0.109375 to 0.109375
- gate_weight: bfloat16 [4, 8192, 3072], P('expert', ('section', 'dp')), may hold values from -0.109375 to 0.109375
- up_weight: bfloat16 [4, 8192, 3072], P('expert', ('section', 'dp')), may hold values from -0.109375 to 0.109375
- down_weight: bfloat16 [4, 8192, 3072], P('expert', ('section', 'dp')), may hold values from -0.0625 to 0.0625
Outputs:
- activations: bfloat16 [2, 4096, 3072], P(None, ('expert', 'dp'), 'section')
- gram: bfloat16 [4, 3072, 3072], P('expert', ('section', 'dp'))
Inputs may be any that keep to these rules, and one draw needn't show every extreme that they name: `routes`: in every micro-batch, each aligned block of 64 tokens (the tokens of one device) names no expert more than 36 times, a bound that some block reaches; the two experts of a token differ; every expert is named somewhere.
All inputs are finite; a program needn't handle non-finite values.
Results may differ from a plain program's by a relative error of at most 0.02.
Values may be sent and summed in bfloat16 or wider, within the bound.
No kernel may reach another device: no remote copies, remote signals or barrier semaphores. Data moves between devices by JAX's collectives and lax.ppermute only.
A program may use at most 128 MiB of HBM per device.

v0:
```python
import jax
import jax.numpy as jnp
from jax import lax
from jax.sharding import PartitionSpec as P


def route_targets(route_ids, experts, capacity):
    onehot = (route_ids[:, :, None] == jnp.arange(experts, dtype=jnp.int32)[None, None, :]).astype(
        jnp.int32
    )
    flattened = onehot.reshape(-1, experts)
    before = jnp.cumsum(flattened, axis=0) - flattened
    slot_rank = jnp.sum(before * flattened, axis=1).reshape(route_ids.shape)
    return route_ids * capacity + slot_rank


def on_device(tokens, routes, router, gate_weight, up_weight, down_weight):
    micro_count = tokens.shape[0]
    rows_dev = tokens.shape[1]
    model_width = tokens.shape[2]
    experts = router.shape[1]
    capacity = 9 * rows_dev // (4 * experts)
    section_count = lax.axis_size("section")
    replicas = lax.axis_size("dp")
    section_index = lax.axis_index("section")
    col_width = model_width // section_count
    gate_rows = gate_weight[0]
    up_rows = up_weight[0]
    down_rows = down_weight[0]
    logits = jnp.einsum("mtd,de->mte", tokens, router, preferred_element_type=jnp.float32)
    chosen = jnp.take_along_axis(logits, routes, axis=-1)
    logit_gap = chosen[..., 0] - chosen[..., 1]
    first_gate = jax.nn.sigmoid(logit_gap)
    second_gate = jax.nn.sigmoid(-logit_gap)
    target = jax.vmap(lambda one_block: route_targets(one_block, experts, capacity))(routes)
    slot_ids = jnp.arange(experts * capacity, dtype=jnp.int32)
    placing = jnp.sum(
        (slot_ids[None, :, None, None] == target[:, None, :, :]).astype(jnp.float32), axis=3
    ).astype(jnp.bfloat16)
    outgoing = jnp.einsum(
        "mst,mtd->msd", placing, tokens, preferred_element_type=jnp.float32
    ).astype(jnp.bfloat16)
    outgoing = outgoing.reshape(micro_count, experts, capacity, model_width)
    arrived = lax.all_to_all(outgoing, "expert", split_axis=1, concat_axis=1, tiled=True)
    rows_all = arrived.reshape(-1, model_width)
    gate_piece = lax.all_gather(gate_rows, "dp", axis=0, tiled=True)
    up_piece = lax.all_gather(up_rows, "dp", axis=0, tiled=True)
    down_piece = lax.all_gather(down_rows, "dp", axis=0, tiled=True)
    gate_part = lax.dot_general(
        rows_all, gate_piece, (((1,), (1,)), ((), ())), preferred_element_type=jnp.float32
    )
    up_part = lax.dot_general(
        rows_all, up_piece, (((1,), (1,)), ((), ())), preferred_element_type=jnp.float32
    )
    inner_units = (jax.nn.silu(gate_part) * up_part).astype(jnp.bfloat16)
    partial_out = jnp.dot(inner_units, down_piece, preferred_element_type=jnp.float32)
    summed_out = lax.psum_scatter(
        partial_out.astype(jnp.bfloat16), "section", scatter_dimension=1, tiled=True
    )
    expert_out = summed_out.reshape(micro_count, experts, capacity, col_width)
    returned = lax.all_to_all(expert_out, "expert", split_axis=1, concat_axis=1, tiled=True)
    flat_back = returned.reshape(micro_count, experts * capacity, col_width)
    first_rows = jnp.take_along_axis(flat_back, target[:, :, 0][:, :, None], axis=1).astype(
        jnp.float32
    )
    second_rows = jnp.take_along_axis(flat_back, target[:, :, 1][:, :, None], axis=1).astype(
        jnp.float32
    )
    own_cols = lax.dynamic_slice_in_dim(tokens, section_index * col_width, col_width, 2).astype(
        jnp.float32
    )
    layer_out = (
        own_cols + first_gate[..., None] * first_rows + second_gate[..., None] * second_rows
    ).astype(jnp.bfloat16)
    all_tokens = rows_dev * lax.axis_size("expert") * replicas
    gram_scale = experts / (2.0 * micro_count * all_tokens)
    block_rows = col_width // replicas
    left_cols = lax.dynamic_slice_in_dim(
        rows_all, section_index * col_width, block_rows * lax.axis_size("dp"), 1
    )
    product = (
        lax.dot_general(
            left_cols, rows_all, (((0,), (0,)), ((), ())), preferred_element_type=jnp.float32
        )
        * gram_scale
    )
    rounded = lax.optimization_barrier(product.astype(jnp.bfloat16))
    gram_block = lax.psum_scatter(
        rounded.astype(jnp.float32).astype(jnp.bfloat16), "dp", scatter_dimension=0, tiled=True
    )
    return (layer_out, gram_block[None])


def solution(mesh):
    return jax.shard_map(
        on_device,
        mesh=mesh,
        in_specs=(
            P(None, ("expert", "dp"), None),
            P(None, ("expert", "dp"), None),
            P(),
            P("expert", ("section", "dp"), None),
            P("expert", ("section", "dp"), None),
            P("expert", ("section", "dp"), None),
        ),
        out_specs=(P(None, ("expert", "dp"), "section"), P("expert", ("section", "dp"), None)),
        check_vma=False,
    )
```

profile of v0, /device:TPU:64, one launch (start us, length us, event | category | flops | bytes accessed | tf_op | source)
XLA Modules:
  0.0 996.9 jit_solution(10317960741379310035)
XLA Ops:
  7.2 0.7 all-gather.7.cloned.1.call-update
  8.0 0.7 all-gather.11.cloned.1.call-update
  8.7 0.7 all-gather.9.cloned.1.call-update
  10.6 0.7 convolution_convert_fusion
  11.2 1.8 copy.70
  13.1 27.1 %all_to_all.10 = bf16[2,4,36,3072]{3,0,2,1:T(2,128)(2,1)S(1)} all-to-all(bf16[2,4,36,3072]{3,0,2,1:T(2,128)(2,1)S(1)} %bitcast.45), channel_id=1, replica_groups=mesh['section'=4,'expert'=4,'dp'=16] {'expert'}, dimensions={1} | all-to-all | bytes 3538944 | tf_op jit(solution)/shard_map/all_to_all | solution.py:44
  40.2 0.4 copy.71
  40.6 1.4 reshape.37
  42.0 241.2 %all-gather.7.cloned.1.call-done = bf16[1,2048,3072]{2,1,0:T(8,128)(2,1)} async-done(((bf16[1,128,3072]{2,1,0:T(8,128)(2,1)}), bf16[1,2048,3072]{2,1,0:T(8,128)(2,1)}) %all-gather.7.cloned.1.call-update) | async-done | bytes 12582928 | tf_op jit(solution)/shard_map/all_gather | solution.py:46
  283.2 10.4 %fusion.4 = f32[288,2048]{1,0:T(8,128)} fusion(bf16[288,3072]{1,0:T(8,128)(2,1)} %reshape.37, bf16[1,2048,3072]{2,1,0:T(8,128)(2,1)} %all-gather.7.cloned.1.call-done), kind=kOutput, calls=%fused_computation.7 | convolution fusion | flops 3623878656 | bytes 16711680 | tf_op jit(solution)/shard_map/dot_general | solution.py:49
  293.5 260.4 %all-gather.11.cloned.1.call-done = bf16[1,2048,3072]{2,1,0:T(8,128)(2,1)} async-done(((bf16[1,128,3072]{2,1,0:T(8,128)(2,1)}), bf16[1,2048,3072]{2,1,0:T(8,128)(2,1)}) %all-gather.11.cloned.1.call-update) | async-done | bytes 12582928 | tf_op jit(solution)/shard_map/all_gather | solution.py:48
  553.9 270.7 %all-gather.9.cloned.1.call-done = bf16[1,2048,3072]{2,1,0:T(8,128)(2,1)} async-done(((bf16[1,128,3072]{2,1,0:T(8,128)(2,1)}), bf16[1,2048,3072]{2,1,0:T(8,128)(2,1)}) %all-gather.9.cloned.1.call-update) | async-done | bytes 12582928 | tf_op jit(solution)/shard_map/all_gather | solution.py:47
  824.6 14.5 %fusion.6 = bf16[288,3072]{1,0:T(8,128)(2,1)} fusion(bf16[1,2048,3072]{2,1,0:T(8,128)(2,1)} %all-gather.11.cloned.1.call-done, bf16[288,3072]{1,0:T(8,128)(2,1)S(1)} %copy-done.2, bf16[1,2048,3072]{2,1,0:T(8,128)(2,1)} %all-gather.9.cloned.1.call-done, f32[288,2048]{1,0:T(8,128)} %fusion.4), kind=kOutput, calls=%fused_computation.11 | convolution fusion | flops 7252180992 | bytes 31064064 | tf_op jit(solution)/shard_map/dot_general | solution.py:56
  839.4 4.4 multiply_convert_fusion
  844.5 2.8 gather_fusion
  847.6 30.8 %reduce-scatter.3.cloned.1.call-done = bf16[288,768]{1,0:T(8,128)(2,1)} async-done(((bf16[288,3072]{1,0:T(8,128)(2,1)}), bf16[288,768]{1,0:T(8,128)(2,1)}) %reduce-scatter.3.cloned.1.call-update) | async-done | bytes 442384 | tf_op jit(solution)/shard_map/reduce_scatter | solution.py:57
  878.3 1.1 reshape.38
  879.4 1.2 copy.72
  880.7 4.3 all-to-all-start.1
  885.2 8.2 all-to-all-done.1
  893.5 1.5 gather_fusion.1
  895.0 1.5 gather_fusion.2
  896.4 0.9 add_convert_fusion
  897.3 93.0 %reduce-scatter.5.cloned.1.call-done = bf16[48,3072]{1,0:T(8,128)(2,1)} async-done(((bf16[768,3072]{1,0:T(8,128)(2,1)}), bf16[48,3072]{1,0:T(8,128)(2,1)}) %reduce-scatter.5.cloned.1.call-update) | async-done | bytes 294928 | tf_op jit(solution)/shard_map/reduce_scatter | solution.py:88
  (38 shorter events, 2.6 us)
Async XLA Ops:
  7.2 836.9 %copy-start = (bf16[3072,4]{0,1:T(4,128)(2,1)S(1)}, bf16[3072,4]{0,1:T(4,128)(2,1)}, u32[]{:S(2)}) copy-start(bf16[3072,4]{0,1:T(4,128)(2,1)} %param.10) | copy-start | bytes 73732
  7.2 2.3 copy-start.3
  7.2 3.4 copy-start.1
  7.2 276.0 %all-gather.7.cloned.1.call-start = ((), (), s32[]{:S(2)}) async-start(), calls=%async_computation.6 | async-start | bytes 13369344 | tf_op jit(solution)/shard_map/all_gather | solution.py:46
  7.9 546.0 %all-gather.11.cloned.1.call-start = ((), (), s32[]{:S(2)}) async-start(), calls=%async_computation.8 | async-start | bytes 13369344 | tf_op jit(solution)/shard_map/all_gather | solution.py:48
  8.7 815.9 %all-gather.9.cloned.1.call-start = ((), (), s32[]{:S(2)}) async-start(), calls=%async_computation.7 | async-start | bytes 13369344 | tf_op jit(solution)/shard_map/all_gather | solution.py:47
  9.4 868.9 %reduce-scatter.3.cloned.1.call-start = ((), (), s32[]{:S(2)}) async-start(), calls=%async_computation.4 | async-start | bytes 2211840 | tf_op jit(solution)/shard_map/reduce_scatter | solution.py:57
  42.0 782.7 %copy-start.2 = (bf16[288,3072]{1,0:T(8,128)(2,1)S(1)}, bf16[288,3072]{1,0:T(8,128)(2,1)}, u32[]{:S(2)}) copy-start(bf16[288,3072]{1,0:T(8,128)(2,1)} %reshape.37) | copy-start | bytes 5308420
  839.2 151.2 %reduce-scatter.5.cloned.1.call-start = ((), (), s32[]{:S(2)}) async-start(), calls=%async_computation.5 | async-start | bytes 5013504 | tf_op jit(solution)/shard_map/reduce_scatter | solution.py:88
  880.7 12.7 %all-to-all-start.1 = ((bf16[2,4,36,768]{3,0,2,1:T(2,128)(2,1)}), bf16[2,4,36,768]{3,0,2,1:T(2,128)(2,1)S(1)}, u32[]{:S(2)}, u32[]{:S(2)}) async-start(bf16[2,4,36,768]{3,0,2,1:T(2,128)(2,1)} %copy.72), calls=%async_computation.2 | async-start | bytes 884736 | tf_op jit(solution)/shard_map/all_to_all | solution.py:61
Sparse Core Ops, SparseCore 0:
  9.8 273.3 all-gather.6
  285.0 268.8 all-gather.10
  555.7 268.8 all-gather.8
  839.3 38.9 reduce-scatter.2
  881.3 109.0 reduce-scatter.4
where the time goes:
time: 998 us; the launch traced here: 997 us
  waiting for transfers between devices  906 us (91%)
  matrix products  30.4 us (3%)
  blocking collectives  27.1 us (3%)
  between operations  14 us (1%)
  local copies, waits for them, and re-layouts  12.9 us (1%)
    all_gather x1, waiting for transfers between devices, on_device(): up_piece = lax.all_gather(up_rows, 'dp', axis=0, tiled=True)  271 us
    all_gather x1, waiting for transfers between devices, on_device(): down_piece = lax.all_gather(down_rows, 'dp', axis=0, tiled=True)  260 us
    all_gather x1, waiting for transfers between devices, on_device(): gate_piece = lax.all_gather(gate_rows, 'dp', axis=0, tiled=True)  241 us
    reduce_scatter x1, waiting for transfers between devices, on_device(): lax.psum_scatter(rounded.astype(jnp.float32).astype(jnp.bfloat16), 'dp',...  93 us
    reduce_scatter x1, waiting for transfers between devices, on_device(): lax.psum_scatter(partial_out.astype(jnp.bfloat16), 'section', scatter_dim...  30.8 us
    all_to_all x1, blocking collectives, on_device(): lax.all_to_all(outgoing, 'expert', split_axis=1, concat_axis=1, tiled=True)  27.1 us
  transfers between devices with their start and end apart: 6, of which 6 were waited for; matrix products, arithmetic and copies ran while one was open for 3% of the time, Pallas kernels for 0%

commit v1 on v0

--- a/solution.py
+++ b/solution.py
@@ -23,29 +23,32 @@
     section_count = lax.axis_size("section")
     replicas = lax.axis_size("dp")
     section_index = lax.axis_index("section")
+    dp_index = lax.axis_index("dp")
     col_width = model_width // section_count
-    gate_rows = gate_weight[0]
-    up_rows = up_weight[0]
-    down_rows = down_weight[0]
+    part = capacity // section_count
     logits = jnp.einsum("mtd,de->mte", tokens, router, preferred_element_type=jnp.float32)
     chosen = jnp.take_along_axis(logits, routes, axis=-1)
     logit_gap = chosen[..., 0] - chosen[..., 1]
     first_gate = jax.nn.sigmoid(logit_gap)
     second_gate = jax.nn.sigmoid(-logit_gap)
     target = jax.vmap(lambda one_block: route_targets(one_block, experts, capacity))(routes)
-    slot_ids = jnp.arange(experts * capacity, dtype=jnp.int32)
+    slot_ids = (
+        jnp.arange(experts, dtype=jnp.int32)[:, None] * capacity
+        + section_index * part
+        + jnp.arange(part, dtype=jnp.int32)[None, :]
+    ).reshape(-1)
     placing = jnp.sum(
         (slot_ids[None, :, None, None] == target[:, None, :, :]).astype(jnp.float32), axis=3
     ).astype(jnp.bfloat16)
     outgoing = jnp.einsum(
         "mst,mtd->msd", placing, tokens, preferred_element_type=jnp.float32
     ).astype(jnp.bfloat16)
-    outgoing = outgoing.reshape(micro_count, experts, capacity, model_width)
+    outgoing = outgoing.reshape(micro_count, experts, part, model_width)
     arrived = lax.all_to_all(outgoing, "expert", split_axis=1, concat_axis=1, tiled=True)
-    rows_all = arrived.reshape(-1, model_width)
-    gate_piece = lax.all_gather(gate_rows, "dp", axis=0, tiled=True)
-    up_piece = lax.all_gather(up_rows, "dp", axis=0, tiled=True)
-    down_piece = lax.all_gather(down_rows, "dp", axis=0, tiled=True)
+    rows_all = lax.all_gather(arrived, "dp", axis=0, tiled=False).reshape(-1, model_width)
+    gate_piece = lax.all_gather(gate_weight[0], "section", axis=0, tiled=True)
+    up_piece = lax.all_gather(up_weight[0], "section", axis=0, tiled=True)
+    down_piece = lax.all_gather(down_weight[0], "section", axis=0, tiled=True)
     gate_part = lax.dot_general(
         rows_all, gate_piece, (((1,), (1,)), ((), ())), preferred_element_type=jnp.float32
     )
@@ -55,9 +58,12 @@
     inner_units = (jax.nn.silu(gate_part) * up_part).astype(jnp.bfloat16)
     partial_out = jnp.dot(inner_units, down_piece, preferred_element_type=jnp.float32)
     summed_out = lax.psum_scatter(
-        partial_out.astype(jnp.bfloat16), "section", scatter_dimension=1, tiled=True
+        partial_out.astype(jnp.bfloat16), "dp", scatter_dimension=0, tiled=True
     )
-    expert_out = summed_out.reshape(micro_count, experts, capacity, col_width)
+    by_cols = summed_out.reshape(micro_count, experts, part, section_count, col_width)
+    by_cols = jnp.moveaxis(by_cols, 3, 0)
+    by_parts = lax.all_to_all(by_cols, "section", split_axis=0, concat_axis=0, tiled=True)
+    expert_out = jnp.moveaxis(by_parts, 0, 2).reshape(micro_count, experts, capacity, col_width)
     returned = lax.all_to_all(expert_out, "expert", split_axis=1, concat_axis=1, tiled=True)
     flat_back = returned.reshape(micro_count, experts * capacity, col_width)
     first_rows = jnp.take_along_axis(flat_back, target[:, :, 0][:, :, None], axis=1).astype(
@@ -76,17 +82,16 @@
     gram_scale = experts / (2.0 * micro_count * all_tokens)
     block_rows = col_width // replicas
     left_cols = lax.dynamic_slice_in_dim(
-        rows_all, section_index * col_width, block_rows * lax.axis_size("dp"), 1
-    )
+        rows_all.reshape(-1, section_count, replicas, block_rows), dp_index, 1, 2
+    ).reshape(-1, section_count * block_rows)
     product = (
         lax.dot_general(
             left_cols, rows_all, (((0,), (0,)), ((), ())), preferred_element_type=jnp.float32
         )
         * gram_scale
     )
-    rounded = lax.optimization_barrier(product.astype(jnp.bfloat16))
     gram_block = lax.psum_scatter(
-        rounded.astype(jnp.float32).astype(jnp.bfloat16), "dp", scatter_dimension=0, tiled=True
+        product.astype(jnp.bfloat16), "section", scatter_dimension=0, tiled=True
     )
     return (layer_out, gram_block[None])
 

time: 998 us -> 509 us (0.51)
  waiting for transfers between devices: 906 us -> 361 us
  local copies, waits for them, and re-layouts: 12.9 us -> 74.8 us
  blocking collectives: 27.1 us -> 12.9 us
    all_gather x3 -> x4, waiting for transfers between devices: 772 us -> 225 us  [the longest x1 155 us: on_device(): lax.all_gather(arrived, 'dp', axis=0, tiled=False).reshape(-1, model_width)]
    another operation x0 -> x1, local copies, waits for them, and re-layouts: none -> 28.4 us  [on_device(): rows_all.reshape(-1, section_count, replicas, block_rows)]
    all_to_all x1, blocking collectives: 27.1 us -> 12.9 us  [on_device(): lax.all_to_all(outgoing, 'expert', split_axis=1, concat_axis=1, tiled=True)]
    reshape x3 -> x4, local copies, waits for them, and re-layouts: 3.74 us -> 17.3 us  [the longest x1 13.8 us: on_device(): lax.all_gather(arrived, 'dp', axis=0, tiled=False).reshape(-1, model_width)]
    all_gather x0 -> x1, local copies, waits for them, and re-layouts: none -> 10.1 us  [on_device(): lax.all_gather(arrived, 'dp', axis=0, tiled=False).reshape(-1, model_width)]
  transfers between devices with their start and end apart: 6 -> 8, of which waited for: 6 -> 8; matrix products, arithmetic and copies ran while one was open for 3% -> 19% of each run, Pallas kernels for 0% -> 0%
where the time goes in v1:
time: 509 us; the launch traced here: 506 us
  waiting for transfers between devices  361 us (71%)
  local copies, waits for them, and re-layouts  74.8 us (15%)
  matrix products  32.9 us (6%)
  between operations  14.3 us (3%)
  blocking collectives  12.9 us (3%)
  starting transfers between devices  7.91 us (2%)
    all_gather x1, waiting for transfers between devices, on_device(): lax.all_gather(arrived, 'dp', axis=0, tiled=False).reshape(-1, model_width)  155 us
    reduce_scatter x1, waiting for transfers between devices, on_device(): lax.psum_scatter(partial_out.astype(jnp.bfloat16), 'dp', scatter_dimensio...  112 us
    all_gather x1, waiting for transfers between devices, on_device(): up_piece = lax.all_gather(up_weight[0], 'section', axis=0, tiled=True)  29.4 us
    another operation x1, local copies, waits for them, and re-layouts, on_device(): rows_all.reshape(-1, section_count, replicas, block_rows)  28.4 us
    all_gather x1, waiting for transfers between devices, on_device(): down_piece = lax.all_gather(down_weight[0], 'section', axis=0, tiled=True)  27.1 us
    reshape x1, local copies, waits for them, and re-layouts, on_device(): lax.all_gather(arrived, 'dp', axis=0, tiled=False).reshape(-1, model_width)  13.8 us
    all_gather x1, waiting for transfers between devices, on_device(): gate_piece = lax.all_gather(gate_weight[0], 'section', axis=0, tiled=True)  13.7 us
    all_to_all x1, blocking collectives, on_device(): lax.all_to_all(outgoing, 'expert', split_axis=1, concat_axis=1, tiled=True)  12.9 us
  transfers between devices with their start and end apart: 8, of which 8 were waited for; matrix products, arithmetic and copies ran while one was open for 19% of the time, Pallas kernels for 0%

profile of v1, /device:TPU:64, one launch (start us, length us, event | category | flops | bytes accessed | tf_op | source)
XLA Modules:
  0.0 506.1 jit_solution(2866995216660940406)
XLA Ops:
  9.9 1.4 convolution_convert_fusion.1
  11.8 12.9 %all_to_all.15 = bf16[2,4,9,3072]{3,0,2,1:T(2,128)(2,1)S(1)} all-to-all(bf16[2,4,9,3072]{3,0,2,1:T(2,128)(2,1)S(1)} %bitcast.47), channel_id=1, replica_groups=mesh['section'=4,'expert'=4,'dp'=16] {'expert'}, dimensions={1} | all-to-all | bytes 884736 | tf_op jit(solution)/shard_map/all_to_all | solution.py:47
  27.7 154.5 %all-gather.9.cloned.1.call-done = bf16[32,4,9,3072]{3,1,2,0:T(4,128)(2,1)} async-done(((bf16[2,4,9,3072]{3,1,2,0:T(4,128)(2,1)}), bf16[32,4,9,3072]{3,1,2,0:T(4,128)(2,1)}) %all-gather.9.cloned.1.call-update) | async-done | bytes 7077904 | tf_op jit(solution)/shard_map/all_gather | solution.py:48
  182.3 10.1 %copy.107 = bf16[32,4,9,3072]{3,2,1,0:T(8,128)(2,1)} copy(bf16[32,4,9,3072]{3,1,2,0:T(4,128)(2,1)} %all-gather.9.cloned.1.call-done) | data formatting | bytes 14155776 | tf_op jit(solution)/shard_map/all_gather | solution.py:48
  192.3 13.8 %reshape.64 = bf16[1152,3072]{1,0:T(8,128)(2,1)} reshape(bf16[32,4,9,3072]{3,2,1,0:T(8,128)(2,1)} %copy.107) | data formatting | bytes 14155776 | tf_op jit(solution)/shard_map/reshape | solution.py:48
  206.2 13.7 %all-gather.11.cloned.1.call-done = bf16[1,512,3072]{2,1,0:T(8,128)(2,1)} async-done(((bf16[1,128,3072]{2,1,0:T(8,128)(2,1)}), bf16[1,512,3072]{2,1,0:T(8,128)(2,1)}) %all-gather.11.cloned.1.call-update) | async-done | bytes 3145744 | tf_op jit(solution)/shard_map/all_gather | solution.py:49
  219.9 7.0 %fusion.3 = f32[1152,512]{1,0:T(8,128)S(1)} fusion(bf16[1152,3072]{1,0:T(8,128)(2,1)} %reshape.64, bf16[1,512,3072]{2,1,0:T(8,128)(2,1)} %all-gather.11.cloned.1.call-done), kind=kOutput, calls=%fused_computation.10 | convolution fusion | flops 3623878656 | bytes 12582912 | tf_op jit(solution)/shard_map/dot_general | solution.py:52
  227.0 29.4 %all-gather.13.cloned.1.call-done = bf16[1,512,3072]{2,1,0:T(8,128)(2,1)} async-done(((bf16[1,128,3072]{2,1,0:T(8,128)(2,1)}), bf16[1,512,3072]{2,1,0:T(8,128)(2,1)}) %all-gather.13.cloned.1.call-update) | async-done | bytes 3145744 | tf_op jit(solution)/shard_map/all_gather | solution.py:50
  256.3 9.2 %fusion.5 = bf16[1152,512]{1,0:T(8,128)(2,1)} fusion(bf16[1152,3072]{1,0:T(8,128)(2,1)} %reshape.64, bf16[1,512,3072]{2,1,0:T(8,128)(2,1)} %all-gather.13.cloned.1.call-done, f32[1152,512]{1,0:T(8,128)S(1)} %fusion.3), kind=kOutput, calls=%fused_computation.12 | convolution fusion | flops 3627417600 | bytes 13762560 | tf_op jit(solution)/shard_map/dot_general | solution.py:55
  265.5 27.1 %all-gather.15.cloned.1.call-done = bf16[1,512,3072]{2,1,0:T(8,128)(2,1)} async-done(((bf16[1,128,3072]{2,1,0:T(8,128)(2,1)}), bf16[1,512,3072]{2,1,0:T(8,128)(2,1)}) %all-gather.15.cloned.1.call-update) | async-done | bytes 3145744 | tf_op jit(solution)/shard_map/all_gather | solution.py:51
  292.6 8.9 %convolution_convert_fusion = bf16[1152,3072]{1,0:T(8,128)(2,1)} fusion(bf16[1152,512]{1,0:T(8,128)(2,1)} %fusion.5, bf16[1,512,3072]{2,1,0:T(8,128)(2,1)} %all-gather.15.cloned.1.call-done), kind=kOutput, calls=%fused_computation.3 | convolution fusion | flops 3627417600 | bytes 11403264 | tf_op jit(solution)/shard_map/dot_general | solution.py:59
  301.7 28.4 %reshape_reshape.3 = bf16[1152,4,16,48]{3,2,1,0:T(8,128)(2,1)} reshape(bf16[32,4,9,3072]{3,2,1,0:T(8,128)(2,1)} %copy.107) | data formatting | bytes 14155776 | tf_op jit(solution)/shard_map/reshape;reshape | solution.py:85
  330.2 6.2 %constant_dynamic-slice_fusion = bf16[1152,4,1,48]{3,2,1,0:T(2,128)(2,1)S(1)} fusion(bf16[1152,4,16,48]{3,2,1,0:T(8,128)(2,1)} %reshape_reshape.3, s32[]{:T(128)S(6)} %select_n.23), kind=kLoop, calls=%fused_computation.41 | loop fusion | bytes 884740 | tf_op jit(solution)/shard_map/dynamic_slice | solution.py:84
  336.4 3.6 copy.114
  340.0 5.9 %fusion = bf16[192,3072]{1,0:T(8,128)(2,1)} fusion(bf16[1152,192]{0,1:T(8,128)(2,1)S(1)} %bitcast.53, bf16[1152,3072]{1,0:T(8,128)(2,1)} %reshape.64), kind=kOutput, calls=%fused_computation.5 | convolution fusion | flops 1360134144 | bytes 8699904 | tf_op jit(solution)/shard_map/dot_general | solution.py:88
  346.5 111.7 %reduce-scatter.3.cloned.1.call-done = bf16[72,3072]{1,0:T(8,128)(2,1)} async-done(((bf16[1152,3072]{1,0:T(8,128)(2,1)}), bf16[72,3072]{1,0:T(8,128)(2,1)}) %reduce-scatter.3.cloned.1.call-update) | async-done | bytes 442384 | tf_op jit(solution)/shard_map/reduce_scatter | solution.py:60
  460.4 3.5 all-to-all-start.1
  464.2 2.8 gather_fusion
  467.2 6.1 %all-to-all-done.1 = bf16[4,2,4,9,768]{4,2,3,1,0:T(4,128)(2,1)S(1)} async-done(((bf16[4,2,4,9,768]{4,2,3,1,0:T(4,128)(2,1)}), bf16[4,2,4,9,768]{4,2,3,1,0:T(4,128)(2,1)S(1)}, u32[]{:S(2)}, u32[]{:S(2)}) %all-to-all-start.1) | async-done | bytes 442400 | tf_op jit(solution)/shard_map/all_to_all | solution.py:65
  474.6 4.0 all-to-all-start.2
  478.8 8.1 %all-to-all-done.2 = bf16[2,4,36,768]{3,0,2,1:T(2,128)(2,1)S(1)} async-done(((bf16[2,4,36,768]{3,0,2,1:T(2,128)(2,1)}), bf16[2,4,36,768]{3,0,2,1:T(2,128)(2,1)S(1)}, u32[]{:S(2)}, u32[]{:S(2)}) %all-to-all-start.2) | async-done | bytes 442400 | tf_op jit(solution)/shard_map/all_to_all | solution.py:67
  487.0 1.5 gather_fusion.2
  488.5 1.5 gather_fusion.1
  490.9 8.4 %reduce-scatter.5.cloned.1.call-done = bf16[48,3072]{1,0:T(8,128)(2,1)} async-done(((bf16[192,3072]{1,0:T(8,128)(2,1)}), bf16[48,3072]{1,0:T(8,128)(2,1)}) %reduce-scatter.5.cloned.1.call-update) | async-done | bytes 294928 | tf_op jit(solution)/shard_map/reduce_scatter | solution.py:93
  (51 shorter events, 12.1 us)
Async XLA Ops:
  7.2 338.9 %copy-start = (bf16[3072,4]{0,1:T(4,128)(2,1)S(1)}, bf16[3072,4]{0,1:T(4,128)(2,1)}, u32[]{:S(2)}) copy-start(bf16[3072,4]{0,1:T(4,128)(2,1)} %param.10) | copy-start | bytes 73732
  7.2 175.1 %all-gather.9.cloned.1.call-start = ((), (), s32[]{:S(2)}) async-start(), calls=%async_computation.7 | async-start | bytes 7520256 | tf_op jit(solution)/shard_map/all_gather | solution.py:48
  25.6 194.3 %all-gather.11.cloned.1.call-start = ((), (), s32[]{:S(2)}) async-start(), calls=%async_computation.8 | async-start | bytes 3932160 | tf_op jit(solution)/shard_map/all_gather | solution.py:49
  26.4 229.9 %all-gather.13.cloned.1.call-start = ((), (), s32[]{:S(2)}) async-start(), calls=%async_computation.9 | async-start | bytes 3932160 | tf_op jit(solution)/shard_map/all_gather | solution.py:50
  27.1 265.5 %all-gather.15.cloned.1.call-start = ((), (), s32[]{:S(2)}) async-start(), calls=%async_computation.10 | async-start | bytes 3932160 | tf_op jit(solution)/shard_map/all_gather | solution.py:51
  27.7 430.4 %reduce-scatter.3.cloned.1.call-start = ((), (), s32[]{:S(2)}) async-start(), calls=%async_computation.5 | async-start | bytes 7520256 | tf_op jit(solution)/shard_map/reduce_scatter | solution.py:60
  301.5 197.8 %reduce-scatter.5.cloned.1.call-start = ((), (), s32[]{:S(2)}) async-start(), calls=%async_computation.6 | async-start | bytes 1474560 | tf_op jit(solution)/shard_map/reduce_scatter | solution.py:93
  340.0 6.0 %copy-start.2 = (s32[2,64,2]{1,2,0:T(2,128)S(1)}, s32[2,64,2]{1,2,0:T(2,128)}, u32[]{:S(2)}) copy-start(s32[2,64,2]{1,2,0:T(2,128)} %param.9) | copy-start | bytes 3076
  340.0 6.0 %copy-start.1 = (bf16[2,64,3072]{2,1,0:T(8,128)(2,1)S(1)}, bf16[2,64,3072]{2,1,0:T(8,128)(2,1)}, u32[]{:S(2)}) copy-start(bf16[2,64,3072]{2,1,0:T(8,128)(2,1)} %param.8) | copy-start | bytes 2359300
  460.4 12.9 %all-to-all-start.1 = ((bf16[4,2,4,9,768]{4,2,3,1,0:T(4,128)(2,1)}), bf16[4,2,4,9,768]{4,2,3,1,0:T(4,128)(2,1)S(1)}, u32[]{:S(2)}, u32[]{:S(2)}) async-start(bf16[4,2,4,9,768]{4,2,3,1,0:T(4,128)(2,1)} %bitcast.46), calls=%async_computation.2 | async-start | bytes 884736 | tf_op jit(solution)/shard_map/all_to_all | solution.py:65
  474.6 12.3 %all-to-all-start.2 = ((bf16[2,4,36,768]{3,0,2,1:T(2,128)(2,1)}), bf16[2,4,36,768]{3,0,2,1:T(2,128)(2,1)S(1)}, u32[]{:S(2)}, u32[]{:S(2)}) async-start(bf16[2,4,36,768]{3,0,2,1:T(2,128)(2,1)} %copy.110), calls=%async_computation.3 | async-start | bytes 884736 | tf_op jit(solution)/shard_map/all_to_all | solution.py:67
Sparse Core Ops, SparseCore 0:
  25.8 156.4 all-gather.8
  184.1 35.7 all-gather.10
  221.7 34.5 all-gather.12
  258.0 34.5 all-gather.14
  301.6 156.4 reduce-scatter.2
  461.4 37.8 reduce-scatter.4

commit v2 on v1

--- a/solution.py
+++ b/solution.py
@@ -45,10 +45,12 @@
     ).astype(jnp.bfloat16)
     outgoing = outgoing.reshape(micro_count, experts, part, model_width)
     arrived = lax.all_to_all(outgoing, "expert", split_axis=1, concat_axis=1, tiled=True)
-    rows_all = lax.all_gather(arrived, "dp", axis=0, tiled=False).reshape(-1, model_width)
-    gate_piece = lax.all_gather(gate_weight[0], "section", axis=0, tiled=True)
-    up_piece = lax.all_gather(up_weight[0], "section", axis=0, tiled=True)
-    down_piece = lax.all_gather(down_weight[0], "section", axis=0, tiled=True)
+    copies = jnp.broadcast_to(arrived[None], (replicas,) + arrived.shape)
+    rows_all = lax.all_to_all(copies, "dp", split_axis=0, concat_axis=0, tiled=True)
+    rows_all = rows_all.reshape(-1, model_width)
+    stacked = jnp.stack([gate_weight[0], up_weight[0], down_weight[0]])
+    pieces = lax.all_gather(stacked, "section", axis=1, tiled=True)
+    gate_piece, up_piece, down_piece = pieces[0], pieces[1], pieces[2]
     gate_part = lax.dot_general(
         rows_all, gate_piece, (((1,), (1,)), ((), ())), preferred_element_type=jnp.float32
     )
@@ -57,9 +59,9 @@
     )
     inner_units = (jax.nn.silu(gate_part) * up_part).astype(jnp.bfloat16)
     partial_out = jnp.dot(inner_units, down_piece, preferred_element_type=jnp.float32)
-    summed_out = lax.psum_scatter(
-        partial_out.astype(jnp.bfloat16), "dp", scatter_dimension=0, tiled=True
-    )
+    chunks = partial_out.astype(jnp.bfloat16).reshape(replicas, -1, model_width)
+    chunks = lax.all_to_all(chunks, "dp", split_axis=0, concat_axis=0, tiled=True)
+    summed_out = jnp.sum(chunks.astype(jnp.float32), axis=0).astype(jnp.bfloat16)
     by_cols = summed_out.reshape(micro_count, experts, part, section_count, col_width)
     by_cols = jnp.moveaxis(by_cols, 3, 0)
     by_parts = lax.all_to_all(by_cols, "section", split_axis=0, concat_axis=0, tiled=True)

time: 509 us -> 442 us (0.87)
  waiting for transfers between devices: 361 us -> 123 us
  blocking collectives: 12.9 us -> 177 us
  matrix products: 32.9 us -> 23.8 us
  other arithmetic: 2.39 us -> 9.41 us
  starting transfers between devices: 7.91 us -> 14.2 us
    all_gather x4 -> x1, waiting for transfers between devices: 225 us -> 0.01 us  [on_device(): pieces = lax.all_gather(stacked, 'section', axis=1, tiled=True)]
    all_to_all x0 -> x1, blocking collectives: none -> 164 us  [on_device(): lax.all_to_all(copies, 'dp', split_axis=0, concat_axis=0, tiled=True)]
    reduce_scatter x1 -> x0, waiting for transfers between devices: 112 us -> none  [on_device(): lax.psum_scatter(partial_out.astype(jnp.bfloat16), 'dp', scatter_dimensio...]
    all_to_all x0 -> x1, waiting for transfers between devices: none -> 109 us  [on_device(): lax.all_to_all(chunks, 'dp', split_axis=0, concat_axis=0, tiled=True)]
    all_gather x1 -> x0, local copies, waits for them, and re-layouts: 10.1 us -> none  [on_device(): lax.all_gather(arrived, 'dp', axis=0, tiled=False).reshape(-1, model_width)]
    reduce_scatter x1, waiting for transfers between devices: 8.43 us -> 0.01 us  [on_device(): lax.psum_scatter(product.astype(jnp.bfloat16), 'section', scatter_dimensi...]
    all_to_all x0 -> x1, local copies, waits for them, and re-layouts: none -> 7.71 us  [on_device(): lax.all_to_all(copies, 'dp', split_axis=0, concat_axis=0, tiled=True)]
    all_to_all x0 -> x1, starting transfers between devices: none -> 6.47 us  [on_device(): lax.all_to_all(chunks, 'dp', split_axis=0, concat_axis=0, tiled=True)]
  transfers between devices with their start and end apart: 8 -> 5, of which waited for: 8 -> 3; matrix products, arithmetic and copies ran while one was open for 19% -> 20% of each run, Pallas kernels for 0% -> 0%
where the time goes in v2:
time: 442 us; the launch traced here: 437 us
  blocking collectives  177 us (40%)
  waiting for transfers between devices  123 us (28%)
  local copies, waits for them, and re-layouts  75.4 us (17%)
  matrix products  23.8 us (5%)
  between operations  14.3 us (3%)
  starting transfers between devices  14.2 us (3%)
  other arithmetic  9.41 us (2%)
    all_to_all x1, blocking collectives, on_device(): lax.all_to_all(copies, 'dp', split_axis=0, concat_axis=0, tiled=True)  164 us
    all_to_all x1, waiting for transfers between devices, on_device(): lax.all_to_all(chunks, 'dp', split_axis=0, concat_axis=0, tiled=True)  109 us
    another operation x1, local copies, waits for them, and re-layouts, on_device(): rows_all.reshape(-1, section_count, replicas, block_rows)  28.4 us
    reshape x1, local copies, waits for them, and re-layouts, on_device(): rows_all = rows_all.reshape(-1, model_width)  13.7 us
    all_to_all x1, blocking collectives, on_device(): lax.all_to_all(outgoing, 'expert', split_axis=1, concat_axis=1, tiled=True)  12.9 us
    dynamic_slice x2, local copies, waits for them, and re-layouts, on_device(): lax.dynamic_slice_in_dim(rows_all.reshape(-1, section_count, replicas, bl...  10.8 us
  transfers between devices with their start and end apart: 5, of which 3 were waited for; matrix products, arithmetic and copies ran while one was open for 20% of the time, Pallas kernels for 0%

profile of v2, /device:TPU:64, one launch (start us, length us, event | category | flops | bytes accessed | tf_op | source)
XLA Modules:
  0.0 437.0 jit_solution(11569183694241379623)
XLA Ops:
  7.2 3.3 pad_maximum_fusion
  12.7 12.9 %all_to_all.25 = bf16[2,4,9,3072]{3,0,2,1:T(2,128)(2,1)S(1)} all-to-all(bf16[2,4,9,3072]{3,0,2,1:T(2,128)(2,1)S(1)} %bitcast.47), channel_id=1, replica_groups=mesh['section'=4,'expert'=4,'dp'=16] {'expert'}, dimensions={1} | all-to-all | bytes 884736 | tf_op jit(solution)/shard_map/all_to_all | solution.py:47
  25.8 3.1 broadcast_in_dim.15
  28.9 163.7 %all_to_all.26 = bf16[16,2,4,9,3072]{4,2,3,1,0:T(4,128)(2,1)S(1)} all-to-all(bf16[16,2,4,9,3072]{4,2,3,1,0:T(4,128)(2,1)S(1)} %broadcast_in_dim.15), channel_id=1, replica_groups=mesh['section'=4,'expert'=4,'dp'=16] {'dp'}, dimensions={0} | all-to-all | bytes 14155776 | tf_op jit(solution)/shard_map/all_to_all | solution.py:49
  192.6 7.7 %copy.105 = bf16[16,2,4,9,3072]{4,3,2,1,0:T(8,128)(2,1)} copy(bf16[16,2,4,9,3072]{4,2,3,1,0:T(4,128)(2,1)S(1)} %all_to_all.26) | data formatting | bytes 14155776 | tf_op jit(solution)/shard_map/all_to_all | solution.py:49
  200.3 13.7 %reshape.68 = bf16[1152,3072]{1,0:T(8,128)(2,1)} reshape(bf16[16,2,4,9,3072]{4,3,2,1,0:T(8,128)(2,1)} %copy.105) | data formatting | bytes 14155776 | tf_op jit(solution)/shard_map/reshape | solution.py:50
  214.1 7.2 %fusion.1 = f32[1152,512]{1,0:T(8,128)S(1)} fusion(bf16[1152,3072]{1,0:T(8,128)(2,1)} %reshape.68, bf16[3,512,3072]{2,1,0:T(8,128)(2,1)} %all-gather.2.cloned.1.call-done), kind=kOutput, calls=%fused_computation.11 | convolution fusion | flops 3623878656 | bytes 12582912 | tf_op jit(solution)/shard_map/dot_general | solution.py:54
  221.3 1.5 copy-done.4
  222.7 4.2 fusion.2
  226.9 5.8 %convolution_convert_fusion = bf16[1152,3072]{1,0:T(8,128)(2,1)} fusion(bf16[1152,512]{1,0:T(8,128)(2,1)S(1)} %fusion.2, bf16[3,512,3072]{2,1,0:T(8,128)(2,1)S(1)} %copy-done.4), kind=kOutput, calls=%fused_computation.3 | convolution fusion | flops 3627417600 | bytes 11403264 | tf_op jit(solution)/shard_map/dot_general | solution.py:61
  232.7 6.5 %all-to-all-start.2 = ((bf16[16,72,3072]{2,1,0:T(8,128)(2,1)}), bf16[16,72,3072]{2,1,0:T(8,128)(2,1)}, u32[]{:S(2)}, u32[]{:S(2)}) async-start(bf16[16,72,3072]{2,1,0:T(8,128)(2,1)} %bitcast.46), calls=%async_computation.2 | async-start | bytes 14155776 | tf_op jit(solution)/shard_map/all_to_all | solution.py:63
  239.5 28.4 %reshape_reshape.3 = bf16[1152,4,16,48]{3,2,1,0:T(8,128)(2,1)} reshape(bf16[16,2,4,9,3072]{4,3,2,1,0:T(8,128)(2,1)} %copy.105) | data formatting | bytes 14155776 | tf_op jit(solution)/shard_map/reshape;reshape | solution.py:87
  267.9 6.1 %constant_dynamic-slice_fusion = bf16[1152,4,1,48]{3,2,1,0:T(2,128)(2,1)S(1)} fusion(bf16[1152,4,16,48]{3,2,1,0:T(8,128)(2,1)} %reshape_reshape.3, s32[]{:T(128)S(6)} %select_n.23), kind=kLoop, calls=%fused_computation.41 | loop fusion | bytes 884740 | tf_op jit(solution)/shard_map/dynamic_slice | solution.py:86
  274.0 4.6 %copy.112 = bf16[1152,4,1,48]{0,3,1,2:T(8,128)(2,1)} copy(bf16[1152,4,1,48]{3,2,1,0:T(2,128)(2,1)S(1)} %constant_dynamic-slice_fusion) | data formatting | bytes 884736 | tf_op jit(solution)/shard_map/dynamic_slice | solution.py:86
  278.7 5.9 %fusion = bf16[192,3072]{1,0:T(8,128)(2,1)} fusion(bf16[1152,192]{0,1:T(8,128)(2,1)} %bitcast.54, bf16[1152,3072]{1,0:T(8,128)(2,1)} %reshape.68), kind=kOutput, calls=%fused_computation.5 | convolution fusion | flops 1360134144 | bytes 8699904 | tf_op jit(solution)/shard_map/dot_general | solution.py:90
  285.0 108.7 %all-to-all-done.2 = bf16[16,72,3072]{2,1,0:T(8,128)(2,1)} async-done(((bf16[16,72,3072]{2,1,0:T(8,128)(2,1)}), bf16[16,72,3072]{2,1,0:T(8,128)(2,1)}, u32[]{:S(2)}, u32[]{:S(2)}) %all-to-all-start.2) | async-done | bytes 7077920 | tf_op jit(solution)/shard_map/all_to_all | solution.py:63
  393.8 4.4 %reduce_sum.32 = bf16[72,3072]{1,0:T(8,128)(2,1)S(1)} reduce(bf16[16,72,3072]{2,1,0:T(8,128)(2,1)} %all-to-all-done.2, bf16[]{:T(256)} %constant.57.clone.1), dimensions={0}, to_apply=%region_3.4 | reduce | flops 3317760 | bytes 7520258 | tf_op jit(solution)/shard_map/reduce_sum | solution.py:64
  399.4 4.0 all-to-all-start.3
  403.7 2.8 gather_fusion
  406.7 6.2 %all-to-all-done.3 = bf16[4,2,4,9,768]{4,2,3,1,0:T(4,128)(2,1)S(1)} async-done(((bf16[4,2,4,9,768]{4,2,3,1,0:T(4,128)(2,1)}), bf16[4,2,4,9,768]{4,2,3,1,0:T(4,128)(2,1)S(1)}, u32[]{:S(2)}, u32[]{:S(2)}) %all-to-all-start.3) | async-done | bytes 442400 | tf_op jit(solution)/shard_map/all_to_all | solution.py:67
  414.2 3.5 all-to-all-start.4
  417.8 8.3 %all-to-all-done.4 = bf16[2,4,36,768]{3,0,2,1:T(2,128)(2,1)S(1)} async-done(((bf16[2,4,36,768]{3,0,2,1:T(2,128)(2,1)}), bf16[2,4,36,768]{3,0,2,1:T(2,128)(2,1)S(1)}, u32[]{:S(2)}, u32[]{:S(2)}) %all-to-all-start.4) | async-done | bytes 442400 | tf_op jit(solution)/shard_map/all_to_all | solution.py:69
  426.2 1.5 gather_fusion.2
  427.7 1.5 gather_fusion.1
  (49 shorter events, 7.2 us)
Async XLA Ops:
  7.2 277.5 %copy-start = (bf16[3072,4]{0,1:T(4,128)(2,1)S(1)}, bf16[3072,4]{0,1:T(4,128)(2,1)}, u32[]{:S(2)}) copy-start(bf16[3072,4]{0,1:T(4,128)(2,1)} %param.10) | copy-start | bytes 73732
  7.2 3.6 copy-start.3
  7.2 4.8 %copy-start.2 = (bf16[2,64,3072]{2,1,0:T(8,128)(2,1)S(1)}, bf16[2,64,3072]{2,1,0:T(8,128)(2,1)}, u32[]{:S(2)}) copy-start(bf16[2,64,3072]{2,1,0:T(8,128)(2,1)} %param.8) | copy-start | bytes 2359300
  7.2 206.8 %all-gather.2.cloned.1.call-start = ((), (), s32[]{:S(2)}) async-start(), calls=%async_computation.6 | async-start | bytes 11796480 | tf_op jit(solution)/shard_map/all_gather | solution.py:52
  214.0 7.2 %copy-start.1 = (bf16[1152,3072]{1,0:T(8,128)(2,1)S(1)}, bf16[1152,3072]{1,0:T(8,128)(2,1)}, u32[]{:S(2)}) copy-start(bf16[1152,3072]{1,0:T(8,128)(2,1)} %reshape.68) | copy-start | bytes 21233668
  214.1 8.7 %copy-start.4 = (bf16[3,512,3072]{2,1,0:T(8,128)(2,1)S(1)}, bf16[3,512,3072]{2,1,0:T(8,128)(2,1)}, u32[]{:S(2)}) copy-start(bf16[3,512,3072]{2,1,0:T(8,128)(2,1)} %all-gather.2.cloned.1.call-done) | copy-start | bytes 28311556
  232.7 161.0 %all-to-all-start.2 = ((bf16[16,72,3072]{2,1,0:T(8,128)(2,1)}), bf16[16,72,3072]{2,1,0:T(8,128)(2,1)}, u32[]{:S(2)}, u32[]{:S(2)}) async-start(bf16[16,72,3072]{2,1,0:T(8,128)(2,1)} %bitcast.46), calls=%async_computation.2 | async-start | bytes 14155776 | tf_op jit(solution)/shard_map/all_to_all | solution.py:63
  239.2 190.9 %reduce-scatter.2.cloned.1.call-start = ((), (), s32[]{:S(2)}) async-start(), calls=%async_computation.7 | async-start | bytes 1474560 | tf_op jit(solution)/shard_map/reduce_scatter | solution.py:95
  399.4 13.5 %all-to-all-start.3 = ((bf16[4,2,4,9,768]{4,2,3,1,0:T(4,128)(2,1)}), bf16[4,2,4,9,768]{4,2,3,1,0:T(4,128)(2,1)S(1)}, u32[]{:S(2)}, u32[]{:S(2)}) async-start(bf16[4,2,4,9,768]{4,2,3,1,0:T(4,128)(2,1)} %copy.106), calls=%async_computation.3 | async-start | bytes 884736 | tf_op jit(solution)/shard_map/all_to_all | solution.py:67
  414.2 12.0 %all-to-all-start.4 = ((bf16[2,4,36,768]{3,0,2,1:T(2,128)(2,1)}), bf16[2,4,36,768]{3,0,2,1:T(2,128)(2,1)S(1)}, u32[]{:S(2)}, u32[]{:S(2)}) async-start(bf16[2,4,36,768]{3,0,2,1:T(2,128)(2,1)} %copy.108), calls=%async_computation.4 | async-start | bytes 884736 | tf_op jit(solution)/shard_map/all_to_all | solution.py:69
Sparse Core Ops, SparseCore 0:
  10.7 120.3 all-gather.1
  284.7 45.1 reduce-scatter.1

commit v3 on v2

--- a/solution.py
+++ b/solution.py
@@ -45,9 +45,20 @@
     ).astype(jnp.bfloat16)
     outgoing = outgoing.reshape(micro_count, experts, part, model_width)
     arrived = lax.all_to_all(outgoing, "expert", split_axis=1, concat_axis=1, tiled=True)
-    copies = jnp.broadcast_to(arrived[None], (replicas,) + arrived.shape)
-    rows_all = lax.all_to_all(copies, "dp", split_axis=0, concat_axis=0, tiled=True)
-    rows_all = rows_all.reshape(-1, model_width)
+    ring = [2 * p if p < replicas // 2 else 2 * (replicas - 1 - p) + 1 for p in range(replicas)]
+    ahead = [(ring[p], ring[(p + 1) % replicas]) for p in range(replicas)]
+    behind = [(ring[p], ring[(p - 1) % replicas]) for p in range(replicas)]
+    half = replicas // 2
+    gathered = [arrived]
+    moving = arrived
+    for _ in range(half):
+        moving = lax.ppermute(moving, "dp", ahead)
+        gathered.append(moving)
+    moving = arrived
+    for _ in range(half - 1):
+        moving = lax.ppermute(moving, "dp", behind)
+        gathered.append(moving)
+    rows_all = jnp.stack(gathered).reshape(-1, model_width)
     stacked = jnp.stack([gate_weight[0], up_weight[0], down_weight[0]])
     pieces = lax.all_gather(stacked, "section", axis=1, tiled=True)
     gate_piece, up_piece, down_piece = pieces[0], pieces[1], pieces[2]
@@ -59,9 +70,20 @@
     )
     inner_units = (jax.nn.silu(gate_part) * up_part).astype(jnp.bfloat16)
     partial_out = jnp.dot(inner_units, down_piece, preferred_element_type=jnp.float32)
-    chunks = partial_out.astype(jnp.bfloat16).reshape(replicas, -1, model_width)
-    chunks = lax.all_to_all(chunks, "dp", split_axis=0, concat_axis=0, tiled=True)
-    summed_out = jnp.sum(chunks.astype(jnp.float32), axis=0).astype(jnp.bfloat16)
+    chunks = partial_out.reshape(replicas, -1, model_width)
+    forward = chunks[half]
+    for k in range(1, half + 1):
+        if k > 1:
+            forward = forward_in.astype(jnp.float32) + chunks[2 * half + 1 - k]
+        forward_in = lax.ppermute(forward.astype(jnp.bfloat16), "dp", ahead)
+    backward = chunks[half - 1]
+    for k in range(1, half):
+        if k > 1:
+            backward = backward_in.astype(jnp.float32) + chunks[half - k]
+        backward_in = lax.ppermute(backward.astype(jnp.bfloat16), "dp", behind)
+    summed_out = (
+        chunks[0] + forward_in.astype(jnp.float32) + backward_in.astype(jnp.float32)
+    ).astype(jnp.bfloat16)
     by_cols = summed_out.reshape(micro_count, experts, part, section_count, col_width)
     by_cols = jnp.moveaxis(by_cols, 3, 0)
     by_parts = lax.all_to_all(by_cols, "section", split_axis=0, concat_axis=0, tiled=True)

time: 442 us -> 397 us (0.90)
  blocking collectives: 177 us -> 12.9 us
  starting transfers between devices: 14.2 us -> 106 us
  waiting for transfers between devices: 123 us -> 133 us
  other arithmetic: 9.41 us -> 18.6 us
  matrix products: 23.8 us -> 29.4 us
    all_to_all x1 -> x0, blocking collectives: 164 us -> none  [on_device(): lax.all_to_all(copies, 'dp', split_axis=0, concat_axis=0, tiled=True)]
    ppermute x0 -> x30, waiting for transfers between devices: none -> 119 us  [the longest x8 57.3 us: on_device(): moving = lax.ppermute(moving, 'dp', ahead)]
    all_to_all x1 -> x0, waiting for transfers between devices: 109 us -> none  [on_device(): lax.all_to_all(chunks, 'dp', split_axis=0, concat_axis=0, tiled=True)]
    ppermute x0 -> x30, starting transfers between devices: none -> 94.7 us  [the longest x7 60.6 us: on_device(): moving = lax.ppermute(moving, 'dp', behind)]
    convert_element_type x0 -> x8, other arithmetic: none -> 13.6 us  [the longest x7 12.2 us: on_device(): forward_in = lax.ppermute(forward.astype(jnp.bfloat16), 'dp', ahead)]
    dot_general x1, matrix products: 5.83 us -> 15.8 us  [on_device(): jnp.dot(inner_units, down_piece, preferred_element_type=jnp.float32)]
    all_to_all x2 -> x0, local copies, waits for them, and re-layouts: 7.88 us -> none  [the longest x1 7.71 us: on_device(): lax.all_to_all(copies, 'dp', split_axis=0, concat_axis=0, tiled=True)]
    another operation x0 -> x2, local copies, waits for them, and re-layouts: none -> 7.2 us  [on_device(): rows_all = jnp.stack(gathered).reshape(-1, model_width)]
  transfers between devices with their start and end apart: 5 -> 34, of which waited for: 3 -> 25; matrix products, arithmetic and copies ran while one was open for 20% -> 22% of each run, Pallas kernels for 0% -> 0%
where the time goes in v3:
time: 397 us; the launch traced here: 390 us
  waiting for transfers between devices  133 us (34%)
  starting transfers between devices  106 us (27%)
  local copies, waits for them, and re-layouts  76.4 us (19%)
  matrix products  29.4 us (7%)
  other arithmetic  18.6 us (5%)
  between operations  14.6 us (4%)
  blocking collectives  12.9 us (3%)
    ppermute x7, starting transfers between devices, on_device(): moving = lax.ppermute(moving, 'dp', behind)  60.6 us
    ppermute x8, waiting for transfers between devices, on_device(): moving = lax.ppermute(moving, 'dp', ahead)  57.3 us
    ppermute x8, waiting for transfers between devices, on_device(): forward_in = lax.ppermute(forward.astype(jnp.bfloat16), 'dp', ahead)  53 us
    another operation x1, local copies, waits for them, and re-layouts, on_device(): rows_all.reshape(-1, section_count, replicas, block_rows)  28.4 us
    ppermute x8, starting transfers between devices, on_device(): forward_in = lax.ppermute(forward.astype(jnp.bfloat16), 'dp', ahead)  19 us
    dot_general x1, matrix products, on_device(): jnp.dot(inner_units, down_piece, preferred_element_type=jnp.float32)  15.8 us
    reshape x1, local copies, waits for them, and re-layouts, on_device(): rows_all = jnp.stack(gathered).reshape(-1, model_width)  13.7 us
    all_to_all x1, blocking collectives, on_device(): lax.all_to_all(outgoing, 'expert', split_axis=1, concat_axis=1, tiled=True)  12.9 us
  transfers between devices with their start and end apart: 34, of which 25 were waited for; matrix products, arithmetic and copies ran while one was open for 22% of the time, Pallas kernels for 0%

profile of v3, /device:TPU:64, one launch (start us, length us, event | category | flops | bytes accessed | tf_op | source)
XLA Modules:
  0.0 390.3 jit_solution(11833376123524762556)
XLA Ops:
  12.7 12.9 %all_to_all.15 = bf16[2,4,9,3072]{3,0,2,1:T(2,128)(2,1)S(1)} all-to-all(bf16[2,4,9,3072]{3,0,2,1:T(2,128)(2,1)S(1)} %bitcast.82), channel_id=1, replica_groups=mesh['section'=4,'expert'=4,'dp'=16] {'expert'}, dimensions={1} | all-to-all | bytes 884736 | tf_op jit(solution)/shard_map/all_to_all | solution.py:47
  27.9 8.1 %collective-permute-done = bf16[2,4,9,3072]{3,0,2,1:T(2,128)(2,1)S(1)} collective-permute-done((bf16[2,4,9,3072]{3,0,2,1:T(2,128)(2,1)S(1)}, bf16[2,4,9,3072]{3,0,2,1:T(2,128)(2,1)S(1)}, u32[]{:S(2)}, u32[]{:S(2)}) %collective-permute-start) | collective-permute-done | bytes 442400 | tf_op jit(solution)/shard_map/ppermute | solution.py:55
  39.5 6.9 %collective-permute-done.1 = bf16[2,4,9,3072]{3,0,2,1:T(2,128)(2,1)S(1)} collective-permute-done((bf16[2,4,9,3072]{3,0,2,1:T(2,128)(2,1)S(1)}, bf16[2,4,9,3072]{3,0,2,1:T(2,128)(2,1)S(1)}, u32[]{:S(2)}, u32[]{:S(2)}) %collective-permute-start.1) | collective-permute-done | bytes 442400 | tf_op jit(solution)/shard_map/ppermute | solution.py:55
  60.3 13.6 %collective-permute-start.11 = (bf16[2,4,9,3072]{3,0,2,1:T(2,128)(2,1)S(1)}, bf16[2,4,9,3072]{3,0,2,1:T(2,128)(2,1)S(1)}, u32[]{:S(2)}, u32[]{:S(2)}) collective-permute-start(bf16[2,4,9,3072]{3,0,2,1:T(2,128)(2,1)S(1)} %collective-permute-done.10), channel_id=1, source_target_pairs={{0,1},{2,0},{4,2},{6,4},{8,6},{10,8},{12,10},{14,12},{15,14},{13,1... | collective-permute-start | bytes 1327112 | tf_op jit(solution)/shard_map/ppermute | solution.py:59
  80.1 15.3 %collective-permute-start.12 = (bf16[2,4,9,3072]{3,0,2,1:T(2,128)(2,1)S(1)}, bf16[2,4,9,3072]{3,0,2,1:T(2,128)(2,1)S(1)}, u32[]{:S(2)}, u32[]{:S(2)}) collective-permute-start(bf16[2,4,9,3072]{3,0,2,1:T(2,128)(2,1)S(1)} %collective-permute-done.11), channel_id=1, source_target_pairs={{0,1},{2,0},{4,2},{6,4},{8,6},{10,8},{12,10},{14,12},{15,14},{13,1... | collective-permute-start | bytes 1327112 | tf_op jit(solution)/shard_map/ppermute | solution.py:59
  101.9 15.4 %collective-permute-start.13 = (bf16[2,4,9,3072]{3,0,2,1:T(2,128)(2,1)S(1)}, bf16[2,4,9,3072]{3,0,2,1:T(2,128)(2,1)S(1)}, u32[]{:S(2)}, u32[]{:S(2)}) collective-permute-start(bf16[2,4,9,3072]{3,0,2,1:T(2,128)(2,1)S(1)} %collective-permute-done.12), channel_id=1, source_target_pairs={{0,1},{2,0},{4,2},{6,4},{8,6},{10,8},{12,10},{14,12},{15,14},{13,1... | collective-permute-start | bytes 1327112 | tf_op jit(solution)/shard_map/ppermute | solution.py:59
  123.5 14.0 %collective-permute-start.14 = (bf16[2,4,9,3072]{3,0,2,1:T(2,128)(2,1)S(1)}, bf16[2,4,9,3072]{3,0,2,1:T(2,128)(2,1)S(1)}, u32[]{:S(2)}, u32[]{:S(2)}) collective-permute-start(bf16[2,4,9,3072]{3,0,2,1:T(2,128)(2,1)S(1)} %collective-permute-done.13), channel_id=1, source_target_pairs={{0,1},{2,0},{4,2},{6,4},{8,6},{10,8},{12,10},{14,12},{15,14},{13,1... | collective-permute-start | bytes 1327112 | tf_op jit(solution)/shard_map/ppermute | solution.py:59
  137.8 10.4 %collective-permute-done.6 = bf16[2,4,9,3072]{3,0,2,1:T(2,128)(2,1)S(1)} collective-permute-done((bf16[2,4,9,3072]{3,0,2,1:T(2,128)(2,1)S(1)}, bf16[2,4,9,3072]{3,0,2,1:T(2,128)(2,1)S(1)}, u32[]{:S(2)}, u32[]{:S(2)}) %collective-permute-start.6) | collective-permute-done | bytes 442400 | tf_op jit(solution)/shard_map/ppermute | solution.py:55
  148.6 8.4 %collective-permute-done.7 = bf16[2,4,9,3072]{3,0,2,1:T(2,128)(2,1)S(1)} collective-permute-done((bf16[2,4,9,3072]{3,0,2,1:T(2,128)(2,1)S(1)}, bf16[2,4,9,3072]{3,0,2,1:T(2,128)(2,1)S(1)}, u32[]{:S(2)}, u32[]{:S(2)}) %collective-permute-start.7) | collective-permute-done | bytes 442400 | tf_op jit(solution)/shard_map/ppermute | solution.py:55
  159.8 6.9 %copy.103 = bf16[16,2,4,9,3072]{4,3,2,1,0:T(8,128)(2,1)} copy(bf16[16,2,4,9,3072]{4,1,3,2,0:T(2,128)(2,1)S(1)} %bitcast_dynamic-update-slice_fusion) | data formatting | bytes 14155776 | tf_op jit(solution)/shard_map/stack | solution.py:61
  166.6 13.7 %reshape.97 = bf16[1152,3072]{1,0:T(8,128)(2,1)} reshape(bf16[16,2,4,9,3072]{4,3,2,1,0:T(8,128)(2,1)} %copy.103) | data formatting | bytes 14155776 | tf_op jit(solution)/shard_map/reshape | solution.py:61
  180.4 7.0 %fusion.2 = f32[1152,512]{1,0:T(8,128)S(1)} fusion(bf16[1152,3072]{1,0:T(8,128)(2,1)} %reshape.97, bf16[3,512,3072]{2,1,0:T(8,128)(2,1)} %all-gather.2.cloned.1.call-done), kind=kOutput, calls=%fused_computation.11 | convolution fusion | flops 3623878656 | bytes 12582912 | tf_op jit(solution)/shard_map/dot_general | solution.py:65
  187.4 15.8 %fusion.25 = (bf16[1152,3072]{1,0:T(8,128)(2,1)}, f32[1152,3072]{1,0:T(8,128)}) fusion(bf16[3,512,3072]{2,1,0:T(8,128)(2,1)} %all-gather.2.cloned.1.call-done, bf16[1152,3072]{1,0:T(8,128)(2,1)} %reshape.97, f32[1152,512]{1,0:T(8,128)S(1)} %fusion.2), kind=kOutput, calls=%fused_computation.89 | convolution fusion | flops 7254835200 | bytes 36962304 | tf_op jit(solution)/shard_map/dot_general | solution.py:72
  206.6 10.5 %collective-permute-done.15 = bf16[72,3072]{1,0:T(8,128)(2,1)S(1)} collective-permute-done((bf16[72,3072]{1,0:T(8,128)(2,1)S(1)}, bf16[72,3072]{1,0:T(8,128)(2,1)S(1)}, u32[]{:S(2)}, u32[]{:S(2)}) %collective-permute-start.15) | collective-permute-done | bytes 442400 | tf_op jit(solution)/shard_map/ppermute | solution.py:78
  218.7 8.0 %collective-permute-done.16 = bf16[72,3072]{1,0:T(8,128)(2,1)S(1)} collective-permute-done((bf16[72,3072]{1,0:T(8,128)(2,1)S(1)}, bf16[72,3072]{1,0:T(8,128)(2,1)S(1)}, u32[]{:S(2)}, u32[]{:S(2)}) %collective-permute-start.16) | collective-permute-done | bytes 442400 | tf_op jit(solution)/shard_map/ppermute | solution.py:78
  228.4 9.2 %collective-permute-start.17 = (bf16[72,3072]{1,0:T(8,128)(2,1)S(1)}, bf16[72,3072]{1,0:T(8,128)(2,1)S(1)}, u32[]{:S(2)}, u32[]{:S(2)}) collective-permute-start(bf16[72,3072]{1,0:T(8,128)(2,1)S(1)} %get-tuple-element.15), channel_id=1, source_target_pairs={{0,2},{2,4},{4,6},{6,8},{8,10},{10,12},{12,14},{14,15},{15,13},{13... | collective-permute-start | bytes 1327112 | tf_op jit(solution)/shard_map/ppermute | solution.py:78
  239.3 9.2 %collective-permute-done.17 = bf16[72,3072]{1,0:T(8,128)(2,1)S(1)} collective-permute-done((bf16[72,3072]{1,0:T(8,128)(2,1)S(1)}, bf16[72,3072]{1,0:T(8,128)(2,1)S(1)}, u32[]{:S(2)}, u32[]{:S(2)}) %collective-permute-start.17) | collective-permute-done | bytes 442400 | tf_op jit(solution)/shard_map/ppermute | solution.py:78
  254.1 9.9 %collective-permute-done.18 = bf16[72,3072]{1,0:T(8,128)(2,1)S(1)} collective-permute-done((bf16[72,3072]{1,0:T(8,128)(2,1)S(1)}, bf16[72,3072]{1,0:T(8,128)(2,1)S(1)}, u32[]{:S(2)}, u32[]{:S(2)}) %collective-permute-start.18) | collective-permute-done | bytes 442400 | tf_op jit(solution)/shard_map/ppermute | solution.py:78
  268.0 9.8 %collective-permute-done.19 = bf16[72,3072]{1,0:T(8,128)(2,1)S(1)} collective-permute-done((bf16[72,3072]{1,0:T(8,128)(2,1)S(1)}, bf16[72,3072]{1,0:T(8,128)(2,1)S(1)}, u32[]{:S(2)}, u32[]{:S(2)}) %collective-permute-start.19) | collective-permute-done | bytes 442400 | tf_op jit(solution)/shard_map/ppermute | solution.py:78
  282.9 28.4 %reshape_reshape.3 = bf16[1152,4,16,48]{3,2,1,0:T(8,128)(2,1)} reshape(bf16[16,2,4,9,3072]{4,3,2,1,0:T(8,128)(2,1)} %copy.103) | data formatting | bytes 14155776 | tf_op jit(solution)/shard_map/reshape;reshape | solution.py:109
  311.3 6.1 %constant_dynamic-slice_fusion = bf16[1152,4,1,48]{3,2,1,0:T(2,128)(2,1)S(1)} fusion(bf16[1152,4,16,48]{3,2,1,0:T(8,128)(2,1)} %reshape_reshape.3, s32[]{:T(128)S(6)} %select_n.23), kind=kLoop, calls=%fused_computation.87 | loop fusion | bytes 884740 | tf_op jit(solution)/shard_map/dynamic_slice | solution.py:108
  356.8 6.2 %all-to-all-done.1 = bf16[4,2,4,9,768]{4,2,3,1,0:T(4,128)(2,1)S(1)} async-done(((bf16[4,2,4,9,768]{4,2,3,1,0:T(4,128)(2,1)}), bf16[4,2,4,9,768]{4,2,3,1,0:T(4,128)(2,1)S(1)}, u32[]{:S(2)}, u32[]{:S(2)}) %all-to-all-start.1) | async-done | bytes 442400 | tf_op jit(solution)/shard_map/all_to_all | solution.py:89
  364.2 6.8 %all-to-all-start.2 = ((bf16[2,4,36,768]{3,0,2,1:T(2,128)(2,1)}), bf16[2,4,36,768]{3,0,2,1:T(2,128)(2,1)S(1)}, u32[]{:S(2)}, u32[]{:S(2)}) async-start(bf16[2,4,36,768]{3,0,2,1:T(2,128)(2,1)} %copy.106), calls=%async_computation.2 | async-start | bytes 884736 | tf_op jit(solution)/shard_map/all_to_all | solution.py:91
  371.2 8.1 %all-to-all-done.2 = bf16[2,4,36,768]{3,0,2,1:T(2,128)(2,1)S(1)} async-done(((bf16[2,4,36,768]{3,0,2,1:T(2,128)(2,1)}), bf16[2,4,36,768]{3,0,2,1:T(2,128)(2,1)S(1)}, u32[]{:S(2)}, u32[]{:S(2)}) %all-to-all-start.2) | async-done | bytes 442400 | tf_op jit(solution)/shard_map/all_to_all | solution.py:91
  (123 shorter events, 115.0 us)
Async XLA Ops:
  7.2 173.2 %all-gather.2.cloned.1.call-start = ((), (), s32[]{:S(2)}) async-start(), calls=%async_computation.4 | async-start | bytes 11796480 | tf_op jit(solution)/shard_map/all_gather | solution.py:63
  10.6 372.7 %reduce-scatter.2.cloned.1.call-start = ((), (), s32[]{:S(2)}) async-start(), calls=%async_computation.5 | async-start | bytes 1474560 | tf_op jit(solution)/shard_map/reduce_scatter | solution.py:117
  27.5 11.6 %collective-permute-start.8 = (bf16[2,4,9,3072]{3,0,2,1:T(2,128)(2,1)S(1)}, bf16[2,4,9,3072]{3,0,2,1:T(2,128)(2,1)S(1)}, u32[]{:S(2)}, u32[]{:S(2)}) collective-permute-start(bf16[2,4,9,3072]{3,0,2,1:T(2,128)(2,1)S(1)} %all_to_all.15), channel_id=1, source_target_pairs={{0,1},{2,0},{4,2},{6,4},{8,6},{10,8},{12,10},{14,12},{15,14},{13,1... | collective-permute-start | bytes 1327112 | tf_op jit(solution)/shard_map/ppermute | solution.py:59
  39.1 10.9 %collective-permute-start.9 = (bf16[2,4,9,3072]{3,0,2,1:T(2,128)(2,1)S(1)}, bf16[2,4,9,3072]{3,0,2,1:T(2,128)(2,1)S(1)}, u32[]{:S(2)}, u32[]{:S(2)}) collective-permute-start(bf16[2,4,9,3072]{3,0,2,1:T(2,128)(2,1)S(1)} %collective-permute-done.8), channel_id=1, source_target_pairs={{0,1},{2,0},{4,2},{6,4},{8,6},{10,8},{12,10},{14,12},{15,14},{13,1... | collective-permute-start | bytes 1327112 | tf_op jit(solution)/shard_map/ppermute | solution.py:59
  46.3 12.2 %collective-permute-start.2 = (bf16[2,4,9,3072]{3,0,2,1:T(2,128)(2,1)S(1)}, bf16[2,4,9,3072]{3,0,2,1:T(2,128)(2,1)S(1)}, u32[]{:S(2)}, u32[]{:S(2)}) collective-permute-start(bf16[2,4,9,3072]{3,0,2,1:T(2,128)(2,1)S(1)} %collective-permute-done.1), channel_id=1, source_target_pairs={{0,2},{2,4},{4,6},{6,8},{8,10},{10,12},{12,14},{14,15},{15,13},{13... | collective-permute-start | bytes 1327112 | tf_op jit(solution)/shard_map/ppermute | solution.py:55
  58.5 21.6 %collective-permute-start.3 = (bf16[2,4,9,3072]{3,0,2,1:T(2,128)(2,1)S(1)}, bf16[2,4,9,3072]{3,0,2,1:T(2,128)(2,1)S(1)}, u32[]{:S(2)}, u32[]{:S(2)}) collective-permute-start(bf16[2,4,9,3072]{3,0,2,1:T(2,128)(2,1)S(1)} %collective-permute-done.2), channel_id=1, source_target_pairs={{0,2},{2,4},{4,6},{6,8},{8,10},{10,12},{12,14},{14,15},{15,13},{13... | collective-permute-start | bytes 1327112 | tf_op jit(solution)/shard_map/ppermute | solution.py:55
  60.3 19.8 %collective-permute-start.11 = (bf16[2,4,9,3072]{3,0,2,1:T(2,128)(2,1)S(1)}, bf16[2,4,9,3072]{3,0,2,1:T(2,128)(2,1)S(1)}, u32[]{:S(2)}, u32[]{:S(2)}) collective-permute-start(bf16[2,4,9,3072]{3,0,2,1:T(2,128)(2,1)S(1)} %collective-permute-done.10), channel_id=1, source_target_pairs={{0,1},{2,0},{4,2},{6,4},{8,6},{10,8},{12,10},{14,12},{15,14},{13,1... | collective-permute-start | bytes 1327112 | tf_op jit(solution)/shard_map/ppermute | solution.py:59
  80.1 21.6 %collective-permute-start.4 = (bf16[2,4,9,3072]{3,0,2,1:T(2,128)(2,1)S(1)}, bf16[2,4,9,3072]{3,0,2,1:T(2,128)(2,1)S(1)}, u32[]{:S(2)}, u32[]{:S(2)}) collective-permute-start(bf16[2,4,9,3072]{3,0,2,1:T(2,128)(2,1)S(1)} %collective-permute-done.3), channel_id=1, source_target_pairs={{0,2},{2,4},{4,6},{6,8},{8,10},{10,12},{12,14},{14,15},{15,13},{13... | collective-permute-start | bytes 1327112 | tf_op jit(solution)/shard_map/ppermute | solution.py:55
  80.1 21.8 %collective-permute-start.12 = (bf16[2,4,9,3072]{3,0,2,1:T(2,128)(2,1)S(1)}, bf16[2,4,9,3072]{3,0,2,1:T(2,128)(2,1)S(1)}, u32[]{:S(2)}, u32[]{:S(2)}) collective-permute-start(bf16[2,4,9,3072]{3,0,2,1:T(2,128)(2,1)S(1)} %collective-permute-done.11), channel_id=1, source_target_pairs={{0,1},{2,0},{4,2},{6,4},{8,6},{10,8},{12,10},{14,12},{15,14},{13,1... | collective-permute-start | bytes 1327112 | tf_op jit(solution)/shard_map/ppermute | solution.py:59
  101.6 21.8 %collective-permute-start.5 = (bf16[2,4,9,3072]{3,0,2,1:T(2,128)(2,1)S(1)}, bf16[2,4,9,3072]{3,0,2,1:T(2,128)(2,1)S(1)}, u32[]{:S(2)}, u32[]{:S(2)}) collective-permute-start(bf16[2,4,9,3072]{3,0,2,1:T(2,128)(2,1)S(1)} %collective-permute-done.4), channel_id=1, source_target_pairs={{0,2},{2,4},{4,6},{6,8},{8,10},{10,12},{12,14},{14,15},{15,13},{13... | collective-permute-start | bytes 1327112 | tf_op jit(solution)/shard_map/ppermute | solution.py:55
  101.9 21.6 %collective-permute-start.13 = (bf16[2,4,9,3072]{3,0,2,1:T(2,128)(2,1)S(1)}, bf16[2,4,9,3072]{3,0,2,1:T(2,128)(2,1)S(1)}, u32[]{:S(2)}, u32[]{:S(2)}) collective-permute-start(bf16[2,4,9,3072]{3,0,2,1:T(2,128)(2,1)S(1)} %collective-permute-done.12), channel_id=1, source_target_pairs={{0,1},{2,0},{4,2},{6,4},{8,6},{10,8},{12,10},{14,12},{15,14},{13,1... | collective-permute-start | bytes 1327112 | tf_op jit(solution)/shard_map/ppermute | solution.py:59
  123.5 24.8 %collective-permute-start.6 = (bf16[2,4,9,3072]{3,0,2,1:T(2,128)(2,1)S(1)}, bf16[2,4,9,3072]{3,0,2,1:T(2,128)(2,1)S(1)}, u32[]{:S(2)}, u32[]{:S(2)}) collective-permute-start(bf16[2,4,9,3072]{3,0,2,1:T(2,128)(2,1)S(1)} %collective-permute-done.5), channel_id=1, source_target_pairs={{0,2},{2,4},{4,6},{6,8},{8,10},{10,12},{12,14},{14,15},{15,13},{13... | collective-permute-start | bytes 1327112 | tf_op jit(solution)/shard_map/ppermute | solution.py:55
  123.5 36.0 %collective-permute-start.14 = (bf16[2,4,9,3072]{3,0,2,1:T(2,128)(2,1)S(1)}, bf16[2,4,9,3072]{3,0,2,1:T(2,128)(2,1)S(1)}, u32[]{:S(2)}, u32[]{:S(2)}) collective-permute-start(bf16[2,4,9,3072]{3,0,2,1:T(2,128)(2,1)S(1)} %collective-permute-done.13), channel_id=1, source_target_pairs={{0,1},{2,0},{4,2},{6,4},{8,6},{10,8},{12,10},{14,12},{15,14},{13,1... | collective-permute-start | bytes 1327112 | tf_op jit(solution)/shard_map/ppermute | solution.py:59
  204.4 12.7 %collective-permute-start.15 = (bf16[72,3072]{1,0:T(8,128)(2,1)S(1)}, bf16[72,3072]{1,0:T(8,128)(2,1)S(1)}, u32[]{:S(2)}, u32[]{:S(2)}) collective-permute-start(bf16[72,3072]{1,0:T(8,128)(2,1)S(1)} %get-tuple-element.17), channel_id=1, source_target_pairs={{0,2},{2,4},{4,6},{6,8},{8,10},{10,12},{12,14},{14,15},{15,13},{13... | collective-permute-start | bytes 1327112 | tf_op jit(solution)/shard_map/ppermute | solution.py:78
  204.5 14.2 %collective-permute-start.23 = (bf16[72,3072]{1,0:T(8,128)(2,1)S(1)}, bf16[72,3072]{1,0:T(8,128)(2,1)S(1)}, u32[]{:S(2)}, u32[]{:S(2)}) collective-permute-start(bf16[72,3072]{1,0:T(8,128)(2,1)S(1)} %get-tuple-element.18), channel_id=1, source_target_pairs={{0,1},{2,0},{4,2},{6,4},{8,6},{10,8},{12,10},{14,12},{15,14},{13,1... | collective-permute-start | bytes 1327112 | tf_op jit(solution)/shard_map/ppermute | solution.py:83
  228.4 20.2 %collective-permute-start.17 = (bf16[72,3072]{1,0:T(8,128)(2,1)S(1)}, bf16[72,3072]{1,0:T(8,128)(2,1)S(1)}, u32[]{:S(2)}, u32[]{:S(2)}) collective-permute-start(bf16[72,3072]{1,0:T(8,128)(2,1)S(1)} %get-tuple-element.15), channel_id=1, source_target_pairs={{0,2},{2,4},{4,6},{6,8},{8,10},{10,12},{12,14},{14,15},{15,13},{13... | collective-permute-start | bytes 1327112 | tf_op jit(solution)/shard_map/ppermute | solution.py:78
  237.5 12.8 %collective-permute-start.24 = (bf16[72,3072]{1,0:T(8,128)(2,1)S(1)}, bf16[72,3072]{1,0:T(8,128)(2,1)S(1)}, u32[]{:S(2)}, u32[]{:S(2)}) collective-permute-start(bf16[72,3072]{1,0:T(8,128)(2,1)S(1)} %get-tuple-element.16), channel_id=1, source_target_pairs={{0,1},{2,0},{4,2},{6,4},{8,6},{10,8},{12,10},{14,12},{15,14},{13,1... | collective-permute-start | bytes 1327112 | tf_op jit(solution)/shard_map/ppermute | solution.py:83
  251.9 12.0 %collective-permute-start.18 = (bf16[72,3072]{1,0:T(8,128)(2,1)S(1)}, bf16[72,3072]{1,0:T(8,128)(2,1)S(1)}, u32[]{:S(2)}, u32[]{:S(2)}) collective-permute-start(bf16[72,3072]{1,0:T(8,128)(2,1)S(1)} %get-tuple-element.13), channel_id=1, source_target_pairs={{0,2},{2,4},{4,6},{6,8},{8,10},{10,12},{12,14},{14,15},{15,13},{13... | collective-permute-start | bytes 1327112 | tf_op jit(solution)/shard_map/ppermute | solution.py:78
  265.9 11.9 %collective-permute-start.19 = (bf16[72,3072]{1,0:T(8,128)(2,1)S(1)}, bf16[72,3072]{1,0:T(8,128)(2,1)S(1)}, u32[]{:S(2)}, u32[]{:S(2)}) collective-permute-start(bf16[72,3072]{1,0:T(8,128)(2,1)S(1)} %get-tuple-element.11), channel_id=1, source_target_pairs={{0,2},{2,4},{4,6},{6,8},{8,10},{10,12},{12,14},{14,15},{15,13},{13... | collective-permute-start | bytes 1327112 | tf_op jit(solution)/shard_map/ppermute | solution.py:78
  267.5 10.7 %collective-permute-start.26 = (bf16[72,3072]{1,0:T(8,128)(2,1)S(1)}, bf16[72,3072]{1,0:T(8,128)(2,1)S(1)}, u32[]{:S(2)}, u32[]{:S(2)}) collective-permute-start(bf16[72,3072]{1,0:T(8,128)(2,1)S(1)} %get-tuple-element.12), channel_id=1, source_target_pairs={{0,1},{2,0},{4,2},{6,4},{8,6},{10,8},{12,10},{14,12},{15,14},{13,1... | collective-permute-start | bytes 1327112 | tf_op jit(solution)/shard_map/ppermute | solution.py:83
  280.8 41.3 %collective-permute-start.20 = (bf16[72,3072]{1,0:T(8,128)(2,1)}, bf16[72,3072]{1,0:T(8,128)(2,1)}, u32[]{:S(2)}, u32[]{:S(2)}) collective-permute-start(bf16[72,3072]{1,0:T(8,128)(2,1)} %get-tuple-element.9), channel_id=1, source_target_pairs={{0,2},{2,4},{4,6},{6,8},{8,10},{10,12},{12,14},{14,15},{15,13},{13... | collective-permute-start | bytes 1327112 | tf_op jit(solution)/shard_map/ppermute | solution.py:78
  282.5 39.6 %collective-permute-start.27 = (bf16[72,3072]{1,0:T(8,128)(2,1)}, bf16[72,3072]{1,0:T(8,128)(2,1)}, u32[]{:S(2)}, u32[]{:S(2)}) collective-permute-start(bf16[72,3072]{1,0:T(8,128)(2,1)} %get-tuple-element.10), channel_id=1, source_target_pairs={{0,1},{2,0},{4,2},{6,4},{8,6},{10,8},{12,10},{14,12},{15,14},{13,1... | collective-permute-start | bytes 1327112 | tf_op jit(solution)/shard_map/ppermute | solution.py:83
  349.5 13.4 %all-to-all-start.1 = ((bf16[4,2,4,9,768]{4,2,3,1,0:T(4,128)(2,1)}), bf16[4,2,4,9,768]{4,2,3,1,0:T(4,128)(2,1)S(1)}, u32[]{:S(2)}, u32[]{:S(2)}) async-start(bf16[4,2,4,9,768]{4,2,3,1,0:T(4,128)(2,1)} %bitcast.81), calls=%async_computation.1 | async-start | bytes 884736 | tf_op jit(solution)/shard_map/all_to_all | solution.py:89
  364.2 15.1 %all-to-all-start.2 = ((bf16[2,4,36,768]{3,0,2,1:T(2,128)(2,1)}), bf16[2,4,36,768]{3,0,2,1:T(2,128)(2,1)S(1)}, u32[]{:S(2)}, u32[]{:S(2)}) async-start(bf16[2,4,36,768]{3,0,2,1:T(2,128)(2,1)} %copy.106), calls=%async_computation.2 | async-start | bytes 884736 | tf_op jit(solution)/shard_map/all_to_all | solution.py:91
  (13 other events, 432.1 us)
Sparse Core Ops, SparseCore 0:
  10.7 73.0 all-gather.1
  332.1 41.1 reduce-scatter.1

commit v4 on v2

v4 whole, which is shorter than its diff:
```python
import jax
import jax.numpy as jnp
from jax import lax
from jax.sharding import Mesh
from jax.sharding import PartitionSpec as P


def route_targets(route_ids, experts, capacity):
    onehot = (route_ids[:, :, None] == jnp.arange(experts, dtype=jnp.int32)[None, None, :]).astype(
        jnp.int32
    )
    flattened = onehot.reshape(-1, experts)
    before = jnp.cumsum(flattened, axis=0) - flattened
    slot_rank = jnp.sum(before * flattened, axis=1).reshape(route_ids.shape)
    return route_ids * capacity + slot_rank


def ring_pairs(count, step):
    return [(i, (i + step) % count) for i in range(count)]


def on_device(tokens, routes, router, gate_weight, up_weight, down_weight):
    micro_count = tokens.shape[0]
    rows_dev = tokens.shape[1]
    model_width = tokens.shape[2]
    experts = router.shape[1]
    capacity = 9 * rows_dev // (4 * experts)
    hi_count = lax.axis_size("xh")
    core_count = lax.axis_size("c")
    z_count = lax.axis_size("z")
    lo_count = lax.axis_size("xl")
    section_count = hi_count * core_count
    replicas = z_count * lo_count
    hi_index = lax.axis_index("xh")
    core_index = lax.axis_index("c")
    z_index = lax.axis_index("z")
    lo_index = lax.axis_index("xl")
    section_index = hi_index * core_count + core_index
    col_width = model_width // section_count
    part = capacity // core_count
    logits = jnp.einsum("mtd,de->mte", tokens, router, preferred_element_type=jnp.float32)
    chosen = jnp.take_along_axis(logits, routes, axis=-1)
    logit_gap = chosen[..., 0] - chosen[..., 1]
    first_gate = jax.nn.sigmoid(logit_gap)
    second_gate = jax.nn.sigmoid(-logit_gap)
    target = jax.vmap(lambda one_block: route_targets(one_block, experts, capacity))(routes)
    slot_ids = (
        jnp.arange(experts, dtype=jnp.int32)[:, None] * capacity
        + core_index * part
        + jnp.arange(part, dtype=jnp.int32)[None, :]
    ).reshape(-1)
    placing = jnp.sum(
        (slot_ids[None, :, None, None] == target[:, None, :, :]).astype(jnp.float32), axis=3
    ).astype(jnp.bfloat16)
    outgoing = jnp.einsum(
        "mst,mtd->msd", placing, tokens, preferred_element_type=jnp.float32
    ).astype(jnp.bfloat16)
    outgoing = outgoing.reshape(micro_count, experts, part, model_width)
    arrived = lax.all_to_all(outgoing, "expert", split_axis=1, concat_axis=1, tiled=True)
    own_chunk = arrived.reshape(-1, model_width)
    stacked = jnp.stack([gate_weight[0], up_weight[0], down_weight[0]])
    pieces = lax.all_gather(stacked, ("c", "xl"), axis=1, tiled=True)
    gate_piece, up_piece, down_piece = pieces[0], pieces[1], pieces[2]
    half = z_count // 2
    ahead = ring_pairs(z_count, 1)
    behind = ring_pairs(z_count, -1)
    gathered = [own_chunk]
    moving = own_chunk
    for _ in range(half):
        moving = lax.ppermute(moving, "z", ahead)
        gathered.append(moving)
    moving = own_chunk
    for _ in range(half - 1):
        moving = lax.ppermute(moving, "z", behind)
        gathered.append(moving)
    rows_all = jnp.concatenate(gathered, axis=0)
    gate_part = lax.dot_general(
        rows_all, gate_piece, (((1,), (1,)), ((), ())), preferred_element_type=jnp.float32
    )
    up_part = lax.dot_general(
        rows_all, up_piece, (((1,), (1,)), ((), ())), preferred_element_type=jnp.float32
    )
    inner_units = (jax.nn.silu(gate_part) * up_part).astype(jnp.bfloat16)
    partial_out = jnp.dot(inner_units, down_piece, preferred_element_type=jnp.float32)
    chunks = partial_out.reshape(z_count, -1, model_width)
    forward = chunks[half]
    for k in range(1, half + 1):
        if k > 1:
            forward = forward_in.astype(jnp.float32) + chunks[2 * half + 1 - k]
        forward_in = lax.ppermute(forward.astype(jnp.bfloat16), "z", ahead)
    backward = chunks[half - 1]
    for k in range(1, half):
        if k > 1:
            backward = backward_in.astype(jnp.float32) + chunks[half - k]
        backward_in = lax.ppermute(backward.astype(jnp.bfloat16), "z", behind)
    summed = chunks[0] + forward_in.astype(jnp.float32) + backward_in.astype(jnp.float32)
    halves = summed.reshape(-1, hi_count, col_width * core_count)
    other = lax.dynamic_index_in_dim(halves, 1 - hi_index, 1, keepdims=False)
    mine = lax.dynamic_index_in_dim(halves, hi_index, 1, keepdims=False)
    swapped = lax.ppermute(other.astype(jnp.bfloat16), "xh", ring_pairs(hi_count, 1))
    own_half = (mine + swapped.astype(jnp.float32)).astype(jnp.bfloat16)
    by_cols = jnp.moveaxis(own_half.reshape(-1, core_count, col_width), 1, 0)
    by_parts = lax.all_to_all(by_cols, "c", split_axis=0, concat_axis=0, tiled=True)
    by_parts = by_parts.reshape(core_count, micro_count, experts, part, col_width)
    expert_out = jnp.moveaxis(by_parts, 0, 2).reshape(micro_count, experts, capacity, col_width)
    returned = lax.all_to_all(expert_out, "expert", split_axis=1, concat_axis=1, tiled=True)
    flat_back = returned.reshape(micro_count, experts * capacity, col_width)
    first_rows = jnp.take_along_axis(flat_back, target[:, :, 0][:, :, None], axis=1).astype(
        jnp.float32
    )
    second_rows = jnp.take_along_axis(flat_back, target[:, :, 1][:, :, None], axis=1).astype(
        jnp.float32
    )
    own_cols = lax.dynamic_slice_in_dim(tokens, section_index * col_width, col_width, 2).astype(
        jnp.float32
    )
    layer_out = (
        own_cols + first_gate[..., None] * first_rows + second_gate[..., None] * second_rows
    ).astype(jnp.bfloat16)
    all_tokens = rows_dev * lax.axis_size("expert") * replicas
    gram_scale = experts / (2.0 * micro_count * all_tokens)
    block_rows = col_width // replicas
    pool_core = jnp.arange(core_count, dtype=jnp.int32)[:, None, None]
    pool_lo = jnp.arange(lo_count, dtype=jnp.int32)[None, :, None]
    gram_cols = (
        (hi_index * core_count + pool_core) * col_width
        + (z_index * lo_count + pool_lo) * block_rows
        + jnp.arange(block_rows, dtype=jnp.int32)[None, None, :]
    ).reshape(-1)
    picker = (jnp.arange(model_width, dtype=jnp.int32)[:, None] == gram_cols[None, :]).astype(
        jnp.bfloat16
    )
    left = jnp.dot(rows_all, picker, preferred_element_type=jnp.float32).astype(jnp.bfloat16)
    product = (
        lax.dot_general(left, rows_all, (((0,), (0,)), ((), ())), preferred_element_type=jnp.float32)
        * gram_scale
    )
    gram_block = lax.psum_scatter(
        product.astype(jnp.bfloat16), ("c", "xl"), scatter_dimension=0, tiled=True
    )
    return (layer_out, gram_block[None])


def solution(mesh):
    section, expert, dp = mesh.devices.shape
    fine = Mesh(
        mesh.devices.reshape(2, section // 2, expert, dp // 2, 2), ("xh", "c", "expert", "z", "xl")
    )
    tokens_spec = P(None, ("expert", "z", "xl"), None)
    weight_spec = P("expert", ("xh", "c", "z", "xl"), None)
    return jax.shard_map(
        on_device,
        mesh=fine,
        in_specs=(tokens_spec, tokens_spec, P(), weight_spec, weight_spec, weight_spec),
        out_specs=(P(None, ("expert", "z", "xl"), ("xh", "c")), weight_spec),
        check_vma=False,
    )
```

time: 442 us -> 371 us (0.84)
  the two profiles are of different devices: /device:TPU:64 before, /device:TPU:38 now
where the time goes in v4:
time: 371 us; the launch traced here: 365 us
  waiting for transfers between devices  224 us (60%)
  matrix products  36.3 us (10%)
  starting transfers between devices  28.5 us (8%)
  local copies, waits for them, and re-layouts  23.7 us (6%)
  blocking collectives  21.9 us (6%)
  other arithmetic  16.2 us (4%)
  between operations  14.8 us (4%)
    ppermute x4, waiting for transfers between devices, on_device(): moving = lax.ppermute(moving, 'z', ahead)  65.5 us
    all_gather x1, waiting for transfers between devices, on_device(): pieces = lax.all_gather(stacked, ('c', 'xl'), axis=1, tiled=True)  64 us
    ppermute x4, waiting for transfers between devices, on_device(): forward_in = lax.ppermute(forward.astype(jnp.bfloat16), 'z', ahead)  61.3 us
    ppermute x1, waiting for transfers between devices, on_device(): lax.ppermute(other.astype(jnp.bfloat16), 'xh', ring_pairs(hi_count, 1))  20.6 us
    all_to_all x1, blocking collectives, on_device(): lax.all_to_all(outgoing, 'expert', split_axis=1, concat_axis=1, tiled=True)  17.6 us
    dot_general x1, matrix products, on_device(): lax.dot_general(left, rows_all, (((0,), (0,)), ((), ())), preferred_eleme...  10.3 us
    dot_general x1, matrix products, on_device(): lax.dot_general(rows_all, gate_piece, (((1,), (1,)), ((), ())), preferred...  9.25 us
    dot_general x1, matrix products, on_device(): lax.dot_general(rows_all, up_piece, (((1,), (1,)), ((), ())), preferred_e...  9.16 us
  transfers between devices with their start and end apart: 18, of which 13 were waited for; matrix products, arithmetic and copies ran while one was open for 11% of the time, Pallas kernels for 0%

profile of v4, /device:TPU:38, one launch (start us, length us, event | category | flops | bytes accessed | tf_op | source)
XLA Modules:
  0.0 365.1 jit_solution(5356195160214226353)
XLA Ops:
  7.2 3.3 pad_maximum_fusion
  13.3 17.6 %all_to_all.15 = bf16[2,4,18,3072]{3,0,2,1:T(2,128)(2,1)S(1)} all-to-all(bf16[2,4,18,3072]{3,0,2,1:T(2,128)(2,1)S(1)} %bitcast.58), channel_id=1, replica_groups=mesh['xh'=2,'c'=2,'expert'=4,'z'=8,'xl'=2] {'expert'}, dimensions={1} | all-to-all | bytes 1769472 | tf_op jit(solution)/shard_map/all_to_all | solution.py:59
  33.4 18.3 %collective-permute-done = bf16[144,3072]{1,0:T(8,128)(2,1)S(1)} collective-permute-done((bf16[144,3072]{1,0:T(8,128)(2,1)S(1)}, bf16[144,3072]{1,0:T(8,128)(2,1)S(1)}, u32[]{:S(2)}, u32[]{:S(2)}) %collective-permute-start) | collective-permute-done | bytes 884768 | tf_op jit(solution)/shard_map/ppermute | solution.py:70
  56.0 17.9 %collective-permute-done.1 = bf16[144,3072]{1,0:T(8,128)(2,1)S(1)} collective-permute-done((bf16[144,3072]{1,0:T(8,128)(2,1)S(1)}, bf16[144,3072]{1,0:T(8,128)(2,1)S(1)}, u32[]{:S(2)}, u32[]{:S(2)}) %collective-permute-start.1) | collective-permute-done | bytes 884768 | tf_op jit(solution)/shard_map/ppermute | solution.py:70
  77.8 16.1 %collective-permute-done.2 = bf16[144,3072]{1,0:T(8,128)(2,1)S(1)} collective-permute-done((bf16[144,3072]{1,0:T(8,128)(2,1)S(1)}, bf16[144,3072]{1,0:T(8,128)(2,1)S(1)}, u32[]{:S(2)}, u32[]{:S(2)}) %collective-permute-start.2) | collective-permute-done | bytes 884768 | tf_op jit(solution)/shard_map/ppermute | solution.py:70
  94.9 3.1 collective-permute-start.6
  100.0 13.1 %collective-permute-done.3 = bf16[144,3072]{1,0:T(8,128)(2,1)S(1)} collective-permute-done((bf16[144,3072]{1,0:T(8,128)(2,1)S(1)}, bf16[144,3072]{1,0:T(8,128)(2,1)S(1)}, u32[]{:S(2)}, u32[]{:S(2)}) %collective-permute-start.3) | collective-permute-done | bytes 884768 | tf_op jit(solution)/shard_map/ppermute | solution.py:70
  117.1 64.0 %all-gather.2.cloned.1.call-done = bf16[3,512,3072]{2,1,0:T(8,128)(2,1)} async-done(((bf16[3,128,3072]{2,1,0:T(8,128)(2,1)}), bf16[3,512,3072]{2,1,0:T(8,128)(2,1)}) %all-gather.2.cloned.1.call-update) | async-done | bytes 9437200 | tf_op jit(solution)/shard_map/all_gather | solution.py:62
  181.1 9.2 %fusion.2 = f32[1152,512]{1,0:T(8,128)} fusion(bf16[1152,3072]{1,0:T(8,128)(2,1)} %constant_dynamic-update-slice_fusion, bf16[3,512,3072]{2,1,0:T(8,128)(2,1)} %all-gather.2.cloned.1.call-done), kind=kOutput, calls=%fused_computation.9 | convolution fusion | flops 3623878656 | bytes 12582912 | tf_op jit(solution)/shard_map/dot_general | solution.py:80
  190.3 9.3 %fusion.3 = f32[1152,512]{1,0:T(8,128)} fusion(bf16[1152,3072]{1,0:T(8,128)(2,1)} %constant_dynamic-update-slice_fusion, bf16[3,512,3072]{2,1,0:T(8,128)(2,1)} %all-gather.2.cloned.1.call-done), kind=kOutput, calls=%fused_computation.11 | convolution fusion | flops 3623878656 | bytes 12582912 | tf_op jit(solution)/shard_map/dot_general | solution.py:77
  199.5 6.7 %fusion.22 = (bf16[1152,3072]{1,0:T(8,128)(2,1)S(1)}, f32[1152,3072]{1,0:T(8,128)S(1)}) fusion(bf16[3,512,3072]{2,1,0:T(8,128)(2,1)} %all-gather.2.cloned.1.call-done, f32[1152,512]{1,0:T(8,128)} %fusion.2, f32[1152,512]{1,0:T(8,128)} %fusion.3), kind=kOutput, calls=%fused_computation.78 | convolution fusion | flops 3630956544 | bytes 29097984 | tf_op jit(solution)/shard_map/dot_general | solution.py:84
  209.5 19.8 %collective-permute-done.7 = bf16[144,3072]{1,0:T(8,128)(2,1)S(1)} collective-permute-done((bf16[144,3072]{1,0:T(8,128)(2,1)S(1)}, bf16[144,3072]{1,0:T(8,128)(2,1)S(1)}, u32[]{:S(2)}, u32[]{:S(2)}) %collective-permute-start.7) | collective-permute-done | bytes 884768 | tf_op jit(solution)/shard_map/ppermute | solution.py:90
  231.4 19.8 %collective-permute-done.8 = bf16[144,3072]{1,0:T(8,128)(2,1)S(1)} collective-permute-done((bf16[144,3072]{1,0:T(8,128)(2,1)S(1)}, bf16[144,3072]{1,0:T(8,128)(2,1)S(1)}, u32[]{:S(2)}, u32[]{:S(2)}) %collective-permute-start.8) | collective-permute-done | bytes 884768 | tf_op jit(solution)/shard_map/ppermute | solution.py:90
  251.1 4.0 %fusion.9 = (bf16[144,3072]{1,0:T(8,128)(2,1)}, bf16[144,3072]{1,0:T(8,128)(2,1)}) fusion(f32[1152,3072]{1,0:T(8,128)} %copy-done.2, bf16[144,3072]{1,0:T(8,128)(2,1)S(1)} %collective-permute-done.8, bf16[144,3072]{1,0:T(8,128)(2,1)} %collective-permute-done.11), kind=kLoop, calls=%fused_computation.24 | loop fusion | flops 2654208 | bytes 7077888 | tf_op jit(solution)/shard_map/convert_element_type | solution.py:90
  262.1 15.0 %collective-permute-done.9 = bf16[144,3072]{1,0:T(8,128)(2,1)S(1)} collective-permute-done((bf16[144,3072]{1,0:T(8,128)(2,1)}, bf16[144,3072]{1,0:T(8,128)(2,1)S(1)}, u32[]{:S(2)}, u32[]{:S(2)}) %collective-permute-start.9) | collective-permute-done | bytes 884768 | tf_op jit(solution)/shard_map/ppermute | solution.py:90
  277.6 3.7 %fusion.8 = (bf16[144,3072]{1,0:T(8,128)(2,1)}, bf16[144,3072]{1,0:T(8,128)(2,1)}) fusion(f32[1152,3072]{1,0:T(8,128)} %copy-done.2, bf16[144,3072]{1,0:T(8,128)(2,1)S(1)} %collective-permute-done.9, bf16[144,3072]{1,0:T(8,128)(2,1)S(1)} %collective-permute-done.12), kind=kLoop, calls=%fused_computation.22 | loop fusion | flops 2654208 | bytes 7077888 | tf_op jit(solution)/shard_map/convert_element_type | solution.py:90
  281.4 3.7 %collective-permute-start.10 = (bf16[144,3072]{1,0:T(8,128)(2,1)}, bf16[144,3072]{1,0:T(8,128)(2,1)S(1)}, u32[]{:S(2)}, u32[]{:S(2)}) collective-permute-start(bf16[144,3072]{1,0:T(8,128)(2,1)} %get-tuple-element.5), channel_id=1, source_target_pairs={{0,2},{2,4},{4,6},{6,8},{8,10},{10,12},{12,14},{14,0},{1,3},{3,5},... | collective-permute-start | bytes 2654216 | tf_op jit(solution)/shard_map/ppermute | solution.py:90
  285.1 10.3 %fusion = bf16[192,3072]{1,0:T(8,128)(2,1)} fusion(bf16[1152,3072]{1,0:T(8,128)(2,1)} %constant_dynamic-update-slice_fusion, s32[192]{0:T(256)S(1)} %add.202), kind=kOutput, calls=%fused_computation.4 | convolution fusion | flops 2719899648 | bytes 8258304 | tf_op jit(solution)/shard_map/dot_general | solution.py:135
  295.4 6.7 %collective-permute-done.10 = bf16[144,3072]{1,0:T(8,128)(2,1)S(1)} collective-permute-done((bf16[144,3072]{1,0:T(8,128)(2,1)}, bf16[144,3072]{1,0:T(8,128)(2,1)S(1)}, u32[]{:S(2)}, u32[]{:S(2)}) %collective-permute-start.10) | collective-permute-done | bytes 884768 | tf_op jit(solution)/shard_map/ppermute | solution.py:90
  305.2 3.1 fusion.11
  314.0 20.6 %collective-permute-done.14 = bf16[144,1536]{1,0:T(8,128)(2,1)S(1)} collective-permute-done((bf16[144,1536]{1,0:T(8,128)(2,1)S(1)}, bf16[144,1536]{1,0:T(8,128)(2,1)S(1)}, u32[]{:S(2)}, u32[]{:S(2)}) %collective-permute-start.14) | collective-permute-done | bytes 442400 | tf_op jit(solution)/shard_map/ppermute | solution.py:100
  334.8 4.3 %all_to_all.16 = bf16[2,144,768]{2,1,0:T(8,128)(2,1)S(1)} all-to-all(bf16[2,144,768]{2,1,0:T(8,128)(2,1)S(1)} %bitcast.61), channel_id=1, replica_groups=mesh['xh'=2,'c'=2,'expert'=4,'z'=8,'xl'=2] {'c'}, dimensions={0} | all-to-all | bytes 884736 | tf_op jit(solution)/shard_map/all_to_all | solution.py:103
  340.7 4.3 %all-to-all-start.2 = ((bf16[2,4,36,768]{3,0,2,1:T(2,128)(2,1)}), bf16[2,4,36,768]{3,0,2,1:T(2,128)(2,1)S(1)}, u32[]{:S(2)}, u32[]{:S(2)}) async-start(bf16[2,4,36,768]{3,0,2,1:T(2,128)(2,1)} %copy.106), calls=%async_computation.2 | async-start | bytes 884736 | tf_op jit(solution)/shard_map/all_to_all | solution.py:106
  345.2 8.7 %all-to-all-done.2 = bf16[2,4,36,768]{3,0,2,1:T(2,128)(2,1)S(1)} async-done(((bf16[2,4,36,768]{3,0,2,1:T(2,128)(2,1)}), bf16[2,4,36,768]{3,0,2,1:T(2,128)(2,1)S(1)}, u32[]{:S(2)}, u32[]{:S(2)}) %all-to-all-start.2) | async-done | bytes 442400 | tf_op jit(solution)/shard_map/all_to_all | solution.py:106
  (91 shorter events, 47.7 us)
Async XLA Ops:
  7.2 251.4 %copy-start = (bf16[3072,4]{0,1:T(4,128)(2,1)S(1)}, bf16[3072,4]{0,1:T(4,128)(2,1)}, u32[]{:S(2)}) copy-start(bf16[3072,4]{0,1:T(4,128)(2,1)} %param.10) | copy-start | bytes 73732
  7.2 3.6 copy-start.4
  7.2 4.7 %copy-start.3 = (bf16[2,64,3072]{2,1,0:T(8,128)(2,1)S(1)}, bf16[2,64,3072]{2,1,0:T(8,128)(2,1)}, u32[]{:S(2)}) copy-start(bf16[2,64,3072]{2,1,0:T(8,128)(2,1)} %param.8) | copy-start | bytes 2359300
  7.2 173.9 %all-gather.2.cloned.1.call-start = ((), (), s32[]{:S(2)}) async-start(), calls=%async_computation.4 | async-start | bytes 11796480 | tf_op jit(solution)/shard_map/all_gather | solution.py:62
  10.6 347.2 %reduce-scatter.2.cloned.1.call-start = ((), (), s32[]{:S(2)}) async-start(), calls=%async_computation.5 | async-start | bytes 1474560 | tf_op jit(solution)/shard_map/reduce_scatter | solution.py:138
  31.4 20.3 %collective-permute-start = (bf16[144,3072]{1,0:T(8,128)(2,1)S(1)}, bf16[144,3072]{1,0:T(8,128)(2,1)S(1)}, u32[]{:S(2)}, u32[]{:S(2)}) collective-permute-start(bf16[144,3072]{1,0:T(8,128)(2,1)S(1)} %reshape.145), channel_id=1, source_target_pairs={{0,2},{2,4},{4,6},{6,8},{8,10},{10,12},{12,14},{14,0},{1,3},{3,5},... | collective-permute-start | bytes 2654216 | tf_op jit(solution)/shard_map/ppermute | solution.py:70
  51.7 22.2 %collective-permute-start.1 = (bf16[144,3072]{1,0:T(8,128)(2,1)S(1)}, bf16[144,3072]{1,0:T(8,128)(2,1)S(1)}, u32[]{:S(2)}, u32[]{:S(2)}) collective-permute-start(bf16[144,3072]{1,0:T(8,128)(2,1)S(1)} %collective-permute-done), channel_id=1, source_target_pairs={{0,2},{2,4},{4,6},{6,8},{8,10},{10,12},{12,14},{14,0},{1,3},{3,5},... | collective-permute-start | bytes 2654216 | tf_op jit(solution)/shard_map/ppermute | solution.py:70
  53.6 20.3 %collective-permute-start.4 = (bf16[144,3072]{1,0:T(8,128)(2,1)S(1)}, bf16[144,3072]{1,0:T(8,128)(2,1)S(1)}, u32[]{:S(2)}, u32[]{:S(2)}) collective-permute-start(bf16[144,3072]{1,0:T(8,128)(2,1)S(1)} %reshape.145), channel_id=1, source_target_pairs={{0,14},{2,0},{4,2},{6,4},{8,6},{10,8},{12,10},{14,12},{1,15},{3,1}... | collective-permute-start | bytes 2654216 | tf_op jit(solution)/shard_map/ppermute | solution.py:74
  73.9 20.0 %collective-permute-start.2 = (bf16[144,3072]{1,0:T(8,128)(2,1)S(1)}, bf16[144,3072]{1,0:T(8,128)(2,1)S(1)}, u32[]{:S(2)}, u32[]{:S(2)}) collective-permute-start(bf16[144,3072]{1,0:T(8,128)(2,1)S(1)} %collective-permute-done.1), channel_id=1, source_target_pairs={{0,2},{2,4},{4,6},{6,8},{8,10},{10,12},{12,14},{14,0},{1,3},{3,5},... | collective-permute-start | bytes 2654216 | tf_op jit(solution)/shard_map/ppermute | solution.py:70
  73.9 21.0 %collective-permute-start.5 = (bf16[144,3072]{1,0:T(8,128)(2,1)S(1)}, bf16[144,3072]{1,0:T(8,128)(2,1)S(1)}, u32[]{:S(2)}, u32[]{:S(2)}) collective-permute-start(bf16[144,3072]{1,0:T(8,128)(2,1)S(1)} %collective-permute-done.4), channel_id=1, source_target_pairs={{0,14},{2,0},{4,2},{6,4},{8,6},{10,8},{12,10},{14,12},{1,15},{3,1}... | collective-permute-start | bytes 2654216 | tf_op jit(solution)/shard_map/ppermute | solution.py:74
  93.9 19.2 %collective-permute-start.3 = (bf16[144,3072]{1,0:T(8,128)(2,1)S(1)}, bf16[144,3072]{1,0:T(8,128)(2,1)S(1)}, u32[]{:S(2)}, u32[]{:S(2)}) collective-permute-start(bf16[144,3072]{1,0:T(8,128)(2,1)S(1)} %collective-permute-done.2), channel_id=1, source_target_pairs={{0,2},{2,4},{4,6},{6,8},{8,10},{10,12},{12,14},{14,0},{1,3},{3,5},... | collective-permute-start | bytes 2654216 | tf_op jit(solution)/shard_map/ppermute | solution.py:70
  94.9 21.2 %collective-permute-start.6 = (bf16[144,3072]{1,0:T(8,128)(2,1)S(1)}, bf16[144,3072]{1,0:T(8,128)(2,1)S(1)}, u32[]{:S(2)}, u32[]{:S(2)}) collective-permute-start(bf16[144,3072]{1,0:T(8,128)(2,1)S(1)} %collective-permute-done.5), channel_id=1, source_target_pairs={{0,14},{2,0},{4,2},{6,4},{8,6},{10,8},{12,10},{14,12},{1,15},{3,1}... | collective-permute-start | bytes 2654216 | tf_op jit(solution)/shard_map/ppermute | solution.py:74
  206.3 23.0 %copy-start.2 = (f32[1152,3072]{1,0:T(8,128)}, f32[1152,3072]{1,0:T(8,128)S(1)}, u32[]{:S(2)}) copy-start(f32[1152,3072]{1,0:T(8,128)S(1)} %get-tuple-element.16) | copy-start | bytes 42467332
  207.5 21.8 %collective-permute-start.7 = (bf16[144,3072]{1,0:T(8,128)(2,1)S(1)}, bf16[144,3072]{1,0:T(8,128)(2,1)S(1)}, u32[]{:S(2)}, u32[]{:S(2)}) collective-permute-start(bf16[144,3072]{1,0:T(8,128)(2,1)S(1)} %get-tuple-element.9), channel_id=1, source_target_pairs={{0,2},{2,4},{4,6},{6,8},{8,10},{10,12},{12,14},{14,0},{1,3},{3,5},... | collective-permute-start | bytes 2654216 | tf_op jit(solution)/shard_map/ppermute | solution.py:90
  209.0 22.4 %collective-permute-start.11 = (bf16[144,3072]{1,0:T(8,128)(2,1)}, bf16[144,3072]{1,0:T(8,128)(2,1)}, u32[]{:S(2)}, u32[]{:S(2)}) collective-permute-start(bf16[144,3072]{1,0:T(8,128)(2,1)} %get-tuple-element.10), channel_id=1, source_target_pairs={{0,14},{2,0},{4,2},{6,4},{8,6},{10,8},{12,10},{14,12},{1,15},{3,1}... | collective-permute-start | bytes 2654216 | tf_op jit(solution)/shard_map/ppermute | solution.py:95
  229.5 21.6 %collective-permute-start.8 = (bf16[144,3072]{1,0:T(8,128)(2,1)S(1)}, bf16[144,3072]{1,0:T(8,128)(2,1)S(1)}, u32[]{:S(2)}, u32[]{:S(2)}) collective-permute-start(bf16[144,3072]{1,0:T(8,128)(2,1)S(1)} %fusion.10), channel_id=1, source_target_pairs={{0,2},{2,4},{4,6},{6,8},{8,10},{10,12},{12,14},{14,0},{1,3},{3,5},... | collective-permute-start | bytes 2654216 | tf_op jit(solution)/shard_map/ppermute | solution.py:90
  255.1 22.0 %collective-permute-start.9 = (bf16[144,3072]{1,0:T(8,128)(2,1)}, bf16[144,3072]{1,0:T(8,128)(2,1)S(1)}, u32[]{:S(2)}, u32[]{:S(2)}) collective-permute-start(bf16[144,3072]{1,0:T(8,128)(2,1)} %get-tuple-element.7), channel_id=1, source_target_pairs={{0,2},{2,4},{4,6},{6,8},{8,10},{10,12},{12,14},{14,0},{1,3},{3,5},... | collective-permute-start | bytes 2654216 | tf_op jit(solution)/shard_map/ppermute | solution.py:90
  256.4 21.3 %collective-permute-start.12 = (bf16[144,3072]{1,0:T(8,128)(2,1)}, bf16[144,3072]{1,0:T(8,128)(2,1)S(1)}, u32[]{:S(2)}, u32[]{:S(2)}) collective-permute-start(bf16[144,3072]{1,0:T(8,128)(2,1)} %get-tuple-element.8), channel_id=1, source_target_pairs={{0,14},{2,0},{4,2},{6,4},{8,6},{10,8},{12,10},{14,12},{1,15},{3,1}... | collective-permute-start | bytes 2654216 | tf_op jit(solution)/shard_map/ppermute | solution.py:95
  281.4 20.8 %collective-permute-start.10 = (bf16[144,3072]{1,0:T(8,128)(2,1)}, bf16[144,3072]{1,0:T(8,128)(2,1)S(1)}, u32[]{:S(2)}, u32[]{:S(2)}) collective-permute-start(bf16[144,3072]{1,0:T(8,128)(2,1)} %get-tuple-element.5), channel_id=1, source_target_pairs={{0,2},{2,4},{4,6},{6,8},{8,10},{10,12},{12,14},{14,0},{1,3},{3,5},... | collective-permute-start | bytes 2654216 | tf_op jit(solution)/shard_map/ppermute | solution.py:90
  285.1 20.1 %collective-permute-start.13 = (bf16[144,3072]{1,0:T(8,128)(2,1)}, bf16[144,3072]{1,0:T(8,128)(2,1)S(1)}, u32[]{:S(2)}, u32[]{:S(2)}) collective-permute-start(bf16[144,3072]{1,0:T(8,128)(2,1)} %get-tuple-element.6), channel_id=1, source_target_pairs={{0,14},{2,0},{4,2},{6,4},{8,6},{10,8},{12,10},{14,12},{1,15},{3,1}... | collective-permute-start | bytes 2654216 | tf_op jit(solution)/shard_map/ppermute | solution.py:95
  311.9 22.7 %collective-permute-start.14 = (bf16[144,1536]{1,0:T(8,128)(2,1)S(1)}, bf16[144,1536]{1,0:T(8,128)(2,1)S(1)}, u32[]{:S(2)}, u32[]{:S(2)}) collective-permute-start(bf16[144,1536]{1,0:T(8,128)(2,1)S(1)} %bitcast.66), channel_id=1, source_target_pairs={{0,128},{128,0},{1,129},{129,1},{2,130},{130,2},{3,131},{131,3},{4... | collective-permute-start | bytes 1327112 | tf_op jit(solution)/shard_map/ppermute | solution.py:100
  339.6 18.2 %copy-start.1 = (bf16[3072,4]{0,1:T(4,128)(2,1)S(1)}, bf16[3072,4]{0,1:T(4,128)(2,1)}, u32[]{:S(2)}) copy-start(bf16[3072,4]{0,1:T(4,128)(2,1)} %param.10) | copy-start | bytes 73732
  340.7 13.2 %all-to-all-start.2 = ((bf16[2,4,36,768]{3,0,2,1:T(2,128)(2,1)}), bf16[2,4,36,768]{3,0,2,1:T(2,128)(2,1)S(1)}, u32[]{:S(2)}, u32[]{:S(2)}) async-start(bf16[2,4,36,768]{3,0,2,1:T(2,128)(2,1)} %copy.106), calls=%async_computation.2 | async-start | bytes 884736 | tf_op jit(solution)/shard_map/all_to_all | solution.py:106
Sparse Core Ops, SparseCore 0:
  10.7 170.3 all-gather.1
  295.5 42.3 reduce-scatter.1
